TPU v7x, 1024 devices: a whole 4x4x32 slice. The times are simulated.
1024 devices in a mesh: expert: 64 (over z, core), dp: 16 (over x, y).
Axes of the slice: x: 4, y: 4, z: 32, core: 2. Of those that a mesh axis runs over, the one named last changes fastest.
Arguments:
- hidden: bfloat16 [16, 64, 64, 8, 768], P('dp', 'expert'), may hold values from -256 to 256, as said below
- expert_ids: int32 [16, 2048, 8], P('dp', 'expert'), may hold values from 0 to 63, all different within a row; in each aligned block of 32 rows (0 to 31, 32 to 63, ..., all dimensions but the last counted through in order) at most 8 rows name the same one
- gate_weights: float32 [16, 2048, 8], P('dp', 'expert'), may hold values from 0.02 to 0.3
- direction: bfloat16 [64, 2048, 768], P('expert'), may hold values from -100 to 100
- solution: float32 [64, 2048, 768], P('expert', 'dp'), may hold values from -6 to 6
- residual: float32 [64, 2048, 768], P('expert', 'dp'), may hold values from -100 to 100
Outputs:
- new_solution: float32 [64, 2048, 768], P('expert', 'dp')
- new_residual: float32 [64, 2048, 768], P('expert', 'dp')
Inputs may be any that keep to these rules, and one draw needn't show every extreme that they name: `expert_ids`: in each aligned block of 32 tokens (the tokens of one device), no expert is named by more than 8 rows, a bound that some block reaches; the 8 ids of a token differ. `hidden`: slots that no row names hold values that reach no output.
All inputs are finite; a program needn't handle non-finite values.
Results may differ from a plain program's by a relative error of at most 0.0095.
Values may be sent and summed in bfloat16 or wider, within the bound.
No kernel may reach another device: no remote copies, remote signals or barrier semaphores. Data moves between devices by JAX's collectives and lax.ppermute only.
A program may use at most 32 MiB of HBM per device.

v0:
```python
import functools

import jax
import jax.numpy as jnp
from jax import lax
from jax.sharding import Mesh
from jax.sharding import PartitionSpec as P

EXPERT = ("expert_0", "expert_1")
DP = ("dp_0", "dp_1")
EXPERT_DP = ("expert_0", "expert_1", "dp_0", "dp_1")


def over_axes(value, axes):
    return functools.reduce(lax.psum, axes, value)


def split_up(value, dim, count):
    before, after = (value.shape[:dim], value.shape[dim + 1 :])
    return jnp.moveaxis(value.reshape(*before, count, -1, *after), dim, 0)


def sent_and_summed(value, axis, dim):
    count = lax.axis_size(axis)
    blocks = lax.all_to_all(split_up(value, dim, count), axis, 0, 0, tiled=True)
    return jnp.sum(blocks.astype(jnp.float32), axis=0)


def slot_numbers(flat_ids, experts):
    onehot = (flat_ids[:, None] == jnp.arange(experts, dtype=jnp.int32)[None, :]).astype(jnp.int32)
    earlier = jnp.cumsum(onehot, axis=0) - onehot
    return jnp.sum(earlier * onehot, axis=1)


def local(hidden, expert_ids, gate_weights, direction, solution, residual):
    sources = hidden.shape[2]
    capacity = hidden.shape[3]
    hidden_units = hidden.shape[4]
    model_width = direction.shape[1]
    tok_rows = expert_ids.shape[1]
    top_count = expert_ids.shape[2]
    experts = lax.axis_size(EXPERT)
    replicas = lax.axis_size(DP)
    shard_rows = model_width // replicas
    norm_scale = 1.0 / (replicas * tok_rows)
    flat_ids = expert_ids.reshape(tok_rows * top_count)
    position = flat_ids * capacity + slot_numbers(flat_ids, experts)
    cached = hidden.reshape(sources * capacity, hidden_units)
    vector = direction.reshape(model_width, hidden_units)
    offset = lax.axis_index(DP) * shard_rows
    own_rows = lax.dynamic_slice_in_dim(vector, offset, shard_rows, 0).astype(jnp.float32)
    residual_rows = residual.reshape(shard_rows, hidden_units)
    images = lax.dot_general(
        cached, vector, (((1,), (1,)), ((), ())), preferred_element_type=jnp.float32
    )
    images = images.astype(jnp.bfloat16).reshape(sources, capacity, model_width)
    returned = lax.all_to_all(images, EXPERT, split_axis=0, concat_axis=0, tiled=True)
    row_images = returned.reshape(experts * capacity, model_width)[position]
    gate_rows = gate_weights.reshape(tok_rows, top_count)
    tangent = jnp.sum(
        gate_rows[:, :, None] * row_images.reshape(tok_rows, top_count, model_width), axis=1
    )
    weighted = (gate_rows[:, :, None] * tangent[:, None, :]).astype(jnp.bfloat16)
    outgoing = jnp.zeros((experts * capacity, model_width), jnp.bfloat16)
    outgoing = outgoing.at[position].set(weighted.reshape(tok_rows * top_count, model_width))
    local_curvature = norm_scale * jnp.sum(tangent * tangent) + jnp.sum(own_rows * own_rows)
    early_sums = (
        over_axes(local_curvature, EXPERT_DP),
        over_axes(jnp.sum(residual_rows * residual_rows), EXPERT_DP),
    )
    arrived = lax.all_to_all(
        outgoing.reshape(experts, capacity, model_width),
        EXPERT,
        split_axis=0,
        concat_axis=0,
        tiled=True,
    )
    arrived = arrived.reshape(sources * capacity, model_width)
    summed = sent_and_summed(
        lax.dot_general(
            arrived, cached, (((0,), (0,)), ((), ())), preferred_element_type=jnp.float32
        ).astype(jnp.bfloat16),
        DP,
        0,
    )
    product = summed * norm_scale + own_rows
    step_size = early_sums[1] / early_sums[0]
    new_solution = solution + step_size * own_rows[None]
    new_residual = residual - step_size * product[None]
    return (new_solution, new_residual)


def solution(mesh):
    torus = Mesh(mesh.devices.reshape(32, 2, 4, 4), ("expert_0", "expert_1", "dp_0", "dp_1"))
    return jax.shard_map(
        local,
        mesh=torus,
        in_specs=(
            P(DP, EXPERT, None, None, None),
            P(DP, EXPERT, None),
            P(DP, EXPERT, None),
            P(EXPERT, None, None),
            P(EXPERT, DP, None),
            P(EXPERT, DP, None),
        ),
        out_specs=(P(EXPERT, DP, None), P(EXPERT, DP, None)),
        check_vma=False,
    )
```

profile of v0, /device:TPU:1, one launch (start us, length us, event | category | flops | bytes accessed | tf_op | source)
XLA Modules:
  0.0 545.6 jit_solution(2881151031464494647)
XLA Ops:
  0.6 0.0 copy-start
  0.6 1.1 copy-done
  1.8 5.1 fusion.5
  6.8 0.0 copy-start.4
  6.8 0.0 copy-start.3
  6.8 30.5 %all-to-all-start = ((bf16[64,8,2048]{2,1,0:T(8,128)(2,1)}), bf16[64,8,2048]{2,1,0:T(8,128)(2,1)S(1)}, u32[]{:S(2)}, u32[]{:S(2)}) async-start(bf16[64,8,2048]{2,1,0:T(8,128)(2,1)} %fusion.5), calls=%async_computation | async-start | bytes 4194304 | tf_op jit(solution)/shard_map/all_to_all | solution.py:57
  37.4 0.0 copy-done.4
  37.4 0.1 copy.17
  37.5 0.1 eq.29
  37.6 0.1 eq.25
  37.7 0.1 copy.16
  37.7 0.1 mul.102
  37.8 0.0 copy-done.3
  37.8 0.1 copy.20
  37.9 0.1 copy.15
  38.0 0.1 mul.112
  38.1 0.6 reduce-window.6
  38.7 0.2 slice_reduce_fusion
  38.9 0.1 fusion.24
  39.1 196.0 %all-to-all-done = bf16[64,8,2048]{2,1,0:T(8,128)(2,1)S(1)} async-done(((bf16[64,8,2048]{2,1,0:T(8,128)(2,1)}), bf16[64,8,2048]{2,1,0:T(8,128)(2,1)S(1)}, u32[]{:S(2)}, u32[]{:S(2)}) %all-to-all-start) | async-done | bytes 2097184 | tf_op jit(solution)/shard_map/all_to_all | solution.py:57
  235.1 2.3 gather_fusion
  237.4 2.2 fusion.8
  239.6 2.9 scatter_custom_fusion
  242.5 203.6 %all_to_all.15 = bf16[64,8,2048]{2,1,0:T(8,128)(2,1)S(1)} all-to-all(bf16[64,8,2048]{2,1,0:T(8,128)(2,1)S(1)} %bitcast.54), channel_id=1, replica_groups=mesh['expert_0'=32,'expert_1'=2,'dp_0'=4,'dp_1'=4] {'expert_0','expert_1'}, dimensions={0} | all-to-all | bytes 4194304 | tf_op jit(solution)/shard_map/all_to_all | solution.py:71
  446.1 3.6 convolution_convert_fusion
  449.7 0.0 copy-start.1
  449.7 6.9 %all-to-all-start.2 = ((bf16[16,128,768]{2,1,0:T(8,128)(2,1)}), bf16[16,128,768]{2,1,0:T(8,128)(2,1)}, u32[]{:S(2)}, u32[]{:S(2)}) async-start(bf16[16,128,768]{2,1,0:T(8,128)(2,1)} %bitcast.55), calls=%async_computation.2 | async-start | bytes 6291456 | tf_op jit(solution)/shard_map/all_to_all | solution.py:25
  456.7 1.6 fusion.18
  458.3 0.0 copy-done.1
  458.3 0.0 copy-start.2
  458.3 0.7 multiply_reduce_fusion
  459.0 0.7 multiply_reduce_fusion.1
  460.9 43.9 %all-reduce = (f32[]{:T(128)}, f32[]{:T(128)}) all-reduce(f32[]{:T(128)} %multiply_reduce_fusion, f32[]{:T(128)S(6)} %add.57), channel_id=1, replica_groups=mesh['expert_0'=32,'expert_1'=2,'dp_0'=4,'dp_1'=4] {'expert_0'}, use_global_device_ids=true, to_apply=%region_1.2 | all-reduce | flops 2 | bytes 16 | tf_op jit(solution)/shard_map/psum | solution.py:15
  504.8 16.7 %all-reduce.3 = (f32[]{:T(128)}, f32[]{:T(128)}) all-reduce(f32[]{:T(128)} %get-tuple-element.2, f32[]{:T(128)} %get-tuple-element.3), channel_id=1, replica_groups=mesh['expert_0'=32,'expert_1'=2,'dp_0'=4,'dp_1'=4] {'expert_1'}, use_global_device_ids=true, to_apply=%region_2.3 | all-reduce | flops 2 | bytes 16 | tf_op jit(solution)/shard_map/psum | solution.py:15
  521.5 9.4 %all-reduce.2 = (f32[]{:T(128)}, f32[]{:T(128)}) all-reduce(f32[]{:T(128)} %get-tuple-element.8, f32[]{:T(128)} %get-tuple-element.9), channel_id=1, replica_groups=mesh['expert_0'=32,'expert_1'=2,'dp_0'=4,'dp_1'=4] {'dp_0'}, use_global_device_ids=true, to_apply=%region_3.4 | all-reduce | flops 2 | bytes 16 | tf_op jit(solution)/shard_map/psum | solution.py:15
  530.9 9.0 %all-reduce.1 = (f32[]{:T(128)}, f32[]{:T(128)}) all-reduce(f32[]{:T(128)} %get-tuple-element.6, f32[]{:T(128)} %get-tuple-element.7), channel_id=1, replica_groups=mesh['expert_0'=32,'expert_1'=2,'dp_0'=4,'dp_1'=4] {'dp_1'}, use_global_device_ids=true, to_apply=%region_4.5 | all-reduce | flops 2 | bytes 16 | tf_op jit(solution)/shard_map/psum | solution.py:15
  541.3 0.0 all-to-all-done.2
  541.3 2.4 convert_reduce_fusion
  543.6 0.0 copy-done.2
  543.6 1.9 fusion.21
  (6 shorter events, 0.1 us)
Async XLA Ops:
  0.6 1.1 copy-start
  6.8 30.5 %copy-start.4 = (s32[1,32,8]{1,2,0:T(8,128)S(1)}, s32[1,32,8]{1,2,0:T(8,128)}, u32[]{:S(2)}) copy-start(s32[1,32,8]{1,2,0:T(8,128)} %param.7) | copy-start | bytes 3076
  6.8 31.0 %copy-start.3 = (f32[1,32,8]{1,2,0:T(8,128)S(1)}, f32[1,32,8]{1,2,0:T(8,128)}, u32[]{:S(2)}) copy-start(f32[1,32,8]{1,2,0:T(8,128)} %param.8) | copy-start | bytes 3076
  6.8 228.3 %all-to-all-start = ((bf16[64,8,2048]{2,1,0:T(8,128)(2,1)}), bf16[64,8,2048]{2,1,0:T(8,128)(2,1)S(1)}, u32[]{:S(2)}, u32[]{:S(2)}) async-start(bf16[64,8,2048]{2,1,0:T(8,128)(2,1)} %fusion.5), calls=%async_computation | async-start | bytes 4194304 | tf_op jit(solution)/shard_map/all_to_all | solution.py:57
  449.7 8.6 %copy-start.1 = (f32[1,128,768]{2,1,0:T(8,128)S(1)}, f32[1,128,768]{2,1,0:T(8,128)}, u32[]{:S(2)}) copy-start(f32[1,128,768]{2,1,0:T(8,128)} %param.11) | copy-start | bytes 1179652
  449.7 91.5 %all-to-all-start.2 = ((bf16[16,128,768]{2,1,0:T(8,128)(2,1)}), bf16[16,128,768]{2,1,0:T(8,128)(2,1)}, u32[]{:S(2)}, u32[]{:S(2)}) async-start(bf16[16,128,768]{2,1,0:T(8,128)(2,1)} %bitcast.55), calls=%async_computation.2 | async-start | bytes 6291456 | tf_op jit(solution)/shard_map/all_to_all | solution.py:25
  458.3 85.3 %copy-start.2 = (f32[1,128,768]{2,1,0:T(8,128)S(1)}, f32[1,128,768]{2,1,0:T(8,128)}, u32[]{:S(2)}) copy-start(f32[1,128,768]{2,1,0:T(8,128)} %param.10) | copy-start | bytes 1179652
where the time goes:
time: 549 us; the launch traced here: 546 us
  blocking collectives  283 us (52%)
  waiting for transfers between devices  196 us (36%)
  starting transfers between devices  37.5 us (7%)
  other arithmetic  13.1 us (2%)
  matrix products  8.64 us (2%)
    all_to_all x1, blocking collectives, local(): lax.all_to_all(outgoing.reshape(experts, capacity, model_width), EXPERT,...  204 us
    all_to_all x1, waiting for transfers between devices, local(): lax.all_to_all(images, EXPERT, split_axis=0, concat_axis=0, tiled=True)  196 us
    psum x4, blocking collectives, over_axes(): return functools.reduce(lax.psum, axes, value)  79 us
    all_to_all x1, starting transfers between devices, local(): lax.all_to_all(images, EXPERT, split_axis=0, concat_axis=0, tiled=True)  30.5 us
  transfers between devices with their start and end apart: 2, of which 1 were waited for; matrix products, arithmetic and copies ran while one was open for 1% of the time, Pallas kernels for 0%

commit v1 on v0

--- a/solution.py
+++ b/solution.py
@@ -64,9 +64,8 @@
     outgoing = jnp.zeros((experts * capacity, model_width), jnp.bfloat16)
     outgoing = outgoing.at[position].set(weighted.reshape(tok_rows * top_count, model_width))
     local_curvature = norm_scale * jnp.sum(tangent * tangent) + jnp.sum(own_rows * own_rows)
-    early_sums = (
-        over_axes(local_curvature, EXPERT_DP),
-        over_axes(jnp.sum(residual_rows * residual_rows), EXPERT_DP),
+    early_sums = lax.psum(
+        jnp.stack([local_curvature, jnp.sum(residual_rows * residual_rows)]), EXPERT_DP
     )
     arrived = lax.all_to_all(
         outgoing.reshape(experts, capacity, model_width),

time: 549 us -> 651 us (1.19)
  blocking collectives: 283 us -> 386 us
    psum x4 -> x1, blocking collectives: 79 us -> 182 us  [local(): lax.psum(jnp.stack([local_curvature, jnp.sum(residual_rows * residual_row...]
where the time goes in v1:
time: 651 us; the launch traced here: 650 us
  blocking collectives  386 us (59%)
  waiting for transfers between devices  196 us (30%)
  starting transfers between devices  37.5 us (6%)
  other arithmetic  13.9 us (2%)
  matrix products  8.64 us (1%)
    all_to_all x1, blocking collectives, local(): lax.all_to_all(outgoing.reshape(experts, capacity, model_width), EXPERT,...  204 us
    all_to_all x1, waiting for transfers between devices, local(): lax.all_to_all(images, EXPERT, split_axis=0, concat_axis=0, tiled=True)  196 us
    psum x1, blocking collectives, local(): lax.psum(jnp.stack([local_curvature, jnp.sum(residual_rows * residual_row...  182 us
    all_to_all x1, starting transfers between devices, local(): lax.all_to_all(images, EXPERT, split_axis=0, concat_axis=0, tiled=True)  30.5 us
  transfers between devices with their start and end apart: 2, of which 1 were waited for; matrix products, arithmetic and copies ran while one was open for 1% of the time, Pallas kernels for 0%

profile of v1, /device:TPU:1, one launch (start us, length us, event | category | flops | bytes accessed | tf_op | source)
XLA Modules:
  0.0 650.2 jit_solution(456171879478893)
XLA Ops:
  0.6 0.0 copy-start
  0.6 1.1 copy-done
  1.8 5.1 fusion.5
  6.8 0.0 copy-start.4
  6.8 0.0 copy-start.3
  6.8 30.5 %all-to-all-start = ((bf16[64,8,2048]{2,1,0:T(8,128)(2,1)}), bf16[64,8,2048]{2,1,0:T(8,128)(2,1)S(1)}, u32[]{:S(2)}, u32[]{:S(2)}) async-start(bf16[64,8,2048]{2,1,0:T(8,128)(2,1)} %fusion.5), calls=%async_computation | async-start | bytes 4194304 | tf_op jit(solution)/shard_map/all_to_all | solution.py:57
  37.4 0.0 copy-done.4
  37.4 0.1 copy.17
  37.5 0.1 eq.29
  37.6 0.1 eq.25
  37.7 0.1 copy.16
  37.7 0.1 mul.101
  37.8 0.0 copy-done.3
  37.8 0.1 copy.20
  37.9 0.1 copy.15
  38.0 0.1 mul.112
  38.1 0.6 reduce-window.6
  38.7 0.2 slice_reduce_fusion
  38.9 0.1 fusion.24
  39.1 196.0 %all-to-all-done = bf16[64,8,2048]{2,1,0:T(8,128)(2,1)S(1)} async-done(((bf16[64,8,2048]{2,1,0:T(8,128)(2,1)}), bf16[64,8,2048]{2,1,0:T(8,128)(2,1)S(1)}, u32[]{:S(2)}, u32[]{:S(2)}) %all-to-all-start) | async-done | bytes 2097184 | tf_op jit(solution)/shard_map/all_to_all | solution.py:57
  235.1 2.3 gather_fusion
  237.4 2.2 fusion.8
  239.6 2.9 scatter_custom_fusion
  242.5 203.6 %all_to_all.15 = bf16[64,8,2048]{2,1,0:T(8,128)(2,1)S(1)} all-to-all(bf16[64,8,2048]{2,1,0:T(8,128)(2,1)S(1)} %bitcast.57), channel_id=1, replica_groups=mesh['expert_0'=32,'expert_1'=2,'dp_0'=4,'dp_1'=4] {'expert_0','expert_1'}, dimensions={0} | all-to-all | bytes 4194304 | tf_op jit(solution)/shard_map/all_to_all | solution.py:70
  446.1 3.6 convolution_convert_fusion
  449.7 0.0 copy-start.1
  449.7 6.9 %all-to-all-start.2 = ((bf16[16,128,768]{2,1,0:T(8,128)(2,1)}), bf16[16,128,768]{2,1,0:T(8,128)(2,1)}, u32[]{:S(2)}, u32[]{:S(2)}) async-start(bf16[16,128,768]{2,1,0:T(8,128)(2,1)} %bitcast.58), calls=%async_computation.2 | async-start | bytes 6291456 | tf_op jit(solution)/shard_map/all_to_all | solution.py:25
  456.7 1.6 fusion.18
  458.3 0.0 copy-done.1
  458.3 0.0 copy-start.2
  458.3 0.7 multiply_reduce_fusion
  459.0 0.7 multiply_reduce_fusion.1
  460.9 0.7 pad_maximum_fusion
  461.6 182.3 %psum.7 = f32[2]{0:T(128)S(1)} all-reduce(f32[2]{0:T(128)S(1)} %pad_maximum_fusion), channel_id=1, replica_groups=mesh['expert_0'=32,'expert_1'=2,'dp_0'=4,'dp_1'=4] {'expert_0','expert_1..., use_global_device_ids=true, to_apply=%region_7.8 | all-reduce | flops 2 | bytes 16 | tf_op jit(solution)/shard_map/psum | solution.py:67
  643.9 0.6 fusion.26
  645.9 0.0 all-to-all-done.2
  645.9 2.4 convert_reduce_fusion
  648.2 0.0 copy-done.2
  648.2 1.9 fusion.21
  (6 shorter events, 0.1 us)
Async XLA Ops:
  0.6 1.1 copy-start
  6.8 30.5 %copy-start.4 = (s32[1,32,8]{1,2,0:T(8,128)S(1)}, s32[1,32,8]{1,2,0:T(8,128)}, u32[]{:S(2)}) copy-start(s32[1,32,8]{1,2,0:T(8,128)} %param.7) | copy-start | bytes 3076
  6.8 31.0 %copy-start.3 = (f32[1,32,8]{1,2,0:T(8,128)S(1)}, f32[1,32,8]{1,2,0:T(8,128)}, u32[]{:S(2)}) copy-start(f32[1,32,8]{1,2,0:T(8,128)} %param.8) | copy-start | bytes 3076
  6.8 228.3 %all-to-all-start = ((bf16[64,8,2048]{2,1,0:T(8,128)(2,1)}), bf16[64,8,2048]{2,1,0:T(8,128)(2,1)S(1)}, u32[]{:S(2)}, u32[]{:S(2)}) async-start(bf16[64,8,2048]{2,1,0:T(8,128)(2,1)} %fusion.5), calls=%async_computation | async-start | bytes 4194304 | tf_op jit(solution)/shard_map/all_to_all | solution.py:57
  449.7 8.6 %copy-start.1 = (f32[1,128,768]{2,1,0:T(8,128)S(1)}, f32[1,128,768]{2,1,0:T(8,128)}, u32[]{:S(2)}) copy-start(f32[1,128,768]{2,1,0:T(8,128)} %param.11) | copy-start | bytes 1179652
  449.7 196.1 %all-to-all-start.2 = ((bf16[16,128,768]{2,1,0:T(8,128)(2,1)}), bf16[16,128,768]{2,1,0:T(8,128)(2,1)}, u32[]{:S(2)}, u32[]{:S(2)}) async-start(bf16[16,128,768]{2,1,0:T(8,128)(2,1)} %bitcast.58), calls=%async_computation.2 | async-start | bytes 6291456 | tf_op jit(solution)/shard_map/all_to_all | solution.py:25
  458.3 189.9 %copy-start.2 = (f32[1,128,768]{2,1,0:T(8,128)S(1)}, f32[1,128,768]{2,1,0:T(8,128)}, u32[]{:S(2)}) copy-start(f32[1,128,768]{2,1,0:T(8,128)} %param.10) | copy-start | bytes 1179652

commit v2 on v1

--- a/solution.py
+++ b/solution.py
@@ -64,17 +64,19 @@
     outgoing = jnp.zeros((experts * capacity, model_width), jnp.bfloat16)
     outgoing = outgoing.at[position].set(weighted.reshape(tok_rows * top_count, model_width))
     local_curvature = norm_scale * jnp.sum(tangent * tangent) + jnp.sum(own_rows * own_rows)
-    early_sums = lax.psum(
-        jnp.stack([local_curvature, jnp.sum(residual_rows * residual_rows)]), EXPERT_DP
+    local_sums = jnp.stack([local_curvature, jnp.sum(residual_rows * residual_rows)])
+    sums_high = local_sums.astype(jnp.bfloat16)
+    sums_low = (local_sums - sums_high.astype(jnp.float32)).astype(jnp.bfloat16)
+    lanes = 128
+    carried = jnp.zeros((experts, capacity, lanes), jnp.bfloat16)
+    carried = carried.at[:, 0, 0:2].set(sums_high).at[:, 0, 2:4].set(sums_low)
+    payload = jnp.concatenate(
+        [outgoing.reshape(experts, capacity, model_width), carried], axis=2
     )
-    arrived = lax.all_to_all(
-        outgoing.reshape(experts, capacity, model_width),
-        EXPERT,
-        split_axis=0,
-        concat_axis=0,
-        tiled=True,
-    )
-    arrived = arrived.reshape(sources * capacity, model_width)
+    arrived_full = lax.all_to_all(payload, EXPERT, split_axis=0, concat_axis=0, tiled=True)
+    pieces = arrived_full[:, 0, model_width : model_width + 4].astype(jnp.float32)
+    expert_sums = jnp.sum(pieces[:, 0:2] + pieces[:, 2:4], axis=0)
+    arrived = arrived_full[:, :, :model_width].reshape(sources * capacity, model_width)
     summed = sent_and_summed(
         lax.dot_general(
             arrived, cached, (((0,), (0,)), ((), ())), preferred_element_type=jnp.float32
@@ -82,6 +84,7 @@
         DP,
         0,
     )
+    early_sums = lax.psum(expert_sums, DP)
     product = summed * norm_scale + own_rows
     step_size = early_sums[1] / early_sums[0]
     new_solution = solution + step_size * own_rows[None]

time: 651 us -> 563 us (0.86)
  blocking collectives: 386 us -> 279 us
  local copies, waits for them, and re-layouts: 4.92 us -> 17.8 us
    psum x1, blocking collectives: 182 us -> 61.6 us  [local(): early_sums = lax.psum(expert_sums, DP)]
    all_to_all x1, blocking collectives: 204 us -> 217 us  [local(): lax.all_to_all(payload, EXPERT, split_axis=0, concat_axis=0, tiled=True)]
    scatter x0 -> x2, local copies, waits for them, and re-layouts: none -> 12.3 us  [local(): carried = carried.at[:, 0, 0:2].set(sums_high).at[:, 0, 2:4].set(sums_low)]
where the time goes in v2:
time: 563 us; the launch traced here: 556 us
  blocking collectives  279 us (50%)
  waiting for transfers between devices  192 us (34%)
  starting transfers between devices  37.3 us (7%)
  local copies, waits for them, and re-layouts  17.8 us (3%)
  other arithmetic  17.7 us (3%)
  matrix products  8.6 us (2%)
    all_to_all x1, blocking collectives, local(): lax.all_to_all(payload, EXPERT, split_axis=0, concat_axis=0, tiled=True)  217 us
    all_to_all x1, waiting for transfers between devices, local(): lax.all_to_all(images, EXPERT, split_axis=0, concat_axis=0, tiled=True)  192 us
    psum x1, blocking collectives, local(): early_sums = lax.psum(expert_sums, DP)  61.6 us
    all_to_all x1, starting transfers between devices, local(): lax.all_to_all(images, EXPERT, split_axis=0, concat_axis=0, tiled=True)  30.5 us
    scatter x2, local copies, waits for them, and re-layouts, local(): carried = carried.at[:, 0, 0:2].set(sums_high).at[:, 0, 2:4].set(sums_low)  12.3 us
  transfers between devices with their start and end apart: 2, of which 1 were waited for; matrix products, arithmetic and copies ran while one was open for 1% of the time, Pallas kernels for 0%

profile of v2, /device:TPU:1, one launch (start us, length us, event | category | flops | bytes accessed | tf_op | source)
XLA Modules:
  0.0 556.0 jit_solution(3416465096405142688)
XLA Ops:
  0.6 0.0 copy-start
  0.6 1.1 copy-done
  1.8 5.1 fusion.5
  6.8 0.0 copy-start.4
  6.8 0.0 copy-start.1
  6.8 0.0 copy-start.3
  6.8 0.0 copy-start.5
  6.8 30.5 %all-to-all-start = ((bf16[64,8,2048]{2,1,0:T(8,128)(2,1)}), bf16[64,8,2048]{2,1,0:T(8,128)(2,1)S(1)}, u32[]{:S(2)}, u32[]{:S(2)}) async-start(bf16[64,8,2048]{2,1,0:T(8,128)(2,1)} %fusion.5), calls=%async_computation | async-start | bytes 4194304 | tf_op jit(solution)/shard_map/all_to_all | solution.py:57
  37.4 0.0 copy-done.4
  37.4 0.1 copy.22
  37.5 0.1 eq.29
  37.6 0.1 eq.25
  37.7 0.0 copy-done.1
  37.7 0.7 multiply_reduce_fusion
  39.0 0.1 copy.21
  39.1 0.1 mul.99
  39.2 0.0 copy-done.3
  39.2 0.1 copy.25
  39.3 0.1 copy.26
  39.4 0.1 mul.101
  39.5 0.6 reduce-window.6
  40.1 0.2 slice_reduce_fusion
  40.3 1.6 fusion.17
  41.9 0.1 fusion.23
  42.1 0.6 fusion.33
  42.7 0.0 copy-done.5
  42.7 0.7 and_reduce_fusion
  43.4 191.7 %all-to-all-done = bf16[64,8,2048]{2,1,0:T(8,128)(2,1)S(1)} async-done(((bf16[64,8,2048]{2,1,0:T(8,128)(2,1)}), bf16[64,8,2048]{2,1,0:T(8,128)(2,1)S(1)}, u32[]{:S(2)}, u32[]{:S(2)}) %all-to-all-start) | async-done | bytes 2097184 | tf_op jit(solution)/shard_map/all_to_all | solution.py:57
  235.1 2.3 gather_fusion
  237.5 2.2 fusion.8
  239.7 0.7 multiply_reduce_fusion.1
  241.7 0.1 fusion.31
  241.7 2.6 broadcast_select_fusion
  244.3 0.7 scatter.21
  245.0 11.6 %scatter.22 = bf16[64,8,128]{2,1,0:T(8,128)(2,1)} dynamic-update-slice(bf16[64,8,128]{2,1,0:T(8,128)(2,1)} %scatter.21, bf16[64,1,2]{2,1,0:T(2,128)(2,1)S(1)} %broadcast.137, s32[]{:T(128)} %constant.75.clone.1, s32[]{:T(128)} %bitcast.15, s32[]{:T(128)} %bitcast.16) | dynamic-update-slice | bytes 516 | tf_op jit(solution)/shard_map/scatter | solution.py:72
  256.6 2.9 scatter_custom_fusion
  259.5 1.1 pad_maximum_fusion
  260.6 217.1 %all_to_all.15 = bf16[64,8,2176]{2,1,0:T(8,128)(2,1)S(1)} all-to-all(bf16[64,8,2176]{2,1,0:T(8,128)(2,1)S(1)} %pad_maximum_fusion), channel_id=1, replica_groups=mesh['expert_0'=32,'expert_1'=2,'dp_0'=4,'dp_1'=4] {'expert_0','expert_1'}, dimensions={0} | all-to-all | bytes 4456448 | tf_op jit(solution)/shard_map/all_to_all | solution.py:76
  477.7 3.5 convolution_convert_fusion
  481.2 6.8 %all-to-all-start.2 = ((bf16[16,128,768]{2,1,0:T(8,128)(2,1)}), bf16[16,128,768]{2,1,0:T(8,128)(2,1)}, u32[]{:S(2)}, u32[]{:S(2)}) async-start(bf16[16,128,768]{2,1,0:T(8,128)(2,1)} %bitcast.65), calls=%async_computation.2 | async-start | bytes 6291456 | tf_op jit(solution)/shard_map/all_to_all | solution.py:25
  488.1 0.0 copy-start.2
  488.1 0.1 fusion.25
  488.2 61.6 %psum.7 = f32[2]{0:T(128)S(1)} all-reduce(f32[2]{0:T(128)S(1)} %fusion.25), channel_id=1, replica_groups=mesh['expert_0'=32,'expert_1'=2,'dp_0'=4,'dp_1'=4] {'dp_0','dp_1'}, use_global_device_ids=true, to_apply=%region_10.11 | all-reduce | flops 2 | bytes 16 | tf_op jit(solution)/shard_map/psum | solution.py:87
  549.8 0.6 fusion.32
  551.7 0.0 all-to-all-done.2
  551.7 2.4 convert_reduce_fusion
  554.1 0.0 copy-done.2
  554.1 1.9 fusion.20
  (9 shorter events, 0.1 us)
Async XLA Ops:
  0.6 1.1 copy-start
  6.8 30.6 %copy-start.4 = (s32[1,32,8]{1,2,0:T(8,128)S(1)}, s32[1,32,8]{1,2,0:T(8,128)}, u32[]{:S(2)}) copy-start(s32[1,32,8]{1,2,0:T(8,128)} %param.11) | copy-start | bytes 3076
  6.8 30.8 %copy-start.1 = (f32[1,128,768]{2,1,0:T(8,128)S(1)}, f32[1,128,768]{2,1,0:T(8,128)}, u32[]{:S(2)}) copy-start(f32[1,128,768]{2,1,0:T(8,128)} %param.15) | copy-start | bytes 1179652
  6.8 32.4 %copy-start.3 = (f32[1,32,8]{1,2,0:T(8,128)S(1)}, f32[1,32,8]{1,2,0:T(8,128)}, u32[]{:S(2)}) copy-start(f32[1,32,8]{1,2,0:T(8,128)} %param.12) | copy-start | bytes 3076
  6.8 35.8 %copy-start.5 = (s32[3]{0:T(128)S(1)}, s32[3]{0:T(128)}, u32[]{:S(2)}) copy-start(s32[3]{0:T(128)} %constant.86.clone.1) | copy-start | bytes 40
  6.8 228.3 %all-to-all-start = ((bf16[64,8,2048]{2,1,0:T(8,128)(2,1)}), bf16[64,8,2048]{2,1,0:T(8,128)(2,1)S(1)}, u32[]{:S(2)}, u32[]{:S(2)}) async-start(bf16[64,8,2048]{2,1,0:T(8,128)(2,1)} %fusion.5), calls=%async_computation | async-start | bytes 4194304 | tf_op jit(solution)/shard_map/all_to_all | solution.py:57
  481.2 70.5 %all-to-all-start.2 = ((bf16[16,128,768]{2,1,0:T(8,128)(2,1)}), bf16[16,128,768]{2,1,0:T(8,128)(2,1)}, u32[]{:S(2)}, u32[]{:S(2)}) async-start(bf16[16,128,768]{2,1,0:T(8,128)(2,1)} %bitcast.65), calls=%async_computation.2 | async-start | bytes 6291456 | tf_op jit(solution)/shard_map/all_to_all | solution.py:25
  488.1 66.0 %copy-start.2 = (f32[1,128,768]{2,1,0:T(8,128)S(1)}, f32[1,128,768]{2,1,0:T(8,128)}, u32[]{:S(2)}) copy-start(f32[1,128,768]{2,1,0:T(8,128)} %param.14) | copy-start | bytes 1179652

commit v3 on v1

--- a/solution.py
+++ b/solution.py
@@ -64,9 +64,9 @@
     outgoing = jnp.zeros((experts * capacity, model_width), jnp.bfloat16)
     outgoing = outgoing.at[position].set(weighted.reshape(tok_rows * top_count, model_width))
     local_curvature = norm_scale * jnp.sum(tangent * tangent) + jnp.sum(own_rows * own_rows)
-    early_sums = lax.psum(
-        jnp.stack([local_curvature, jnp.sum(residual_rows * residual_rows)]), EXPERT_DP
-    )
+    local_sums = jnp.stack([local_curvature, jnp.sum(residual_rows * residual_rows)])
+    gathered = lax.all_gather(local_sums, EXPERT, axis=0, tiled=True)
+    expert_sums = jnp.sum(gathered.reshape(experts, 2), axis=0)
     arrived = lax.all_to_all(
         outgoing.reshape(experts, capacity, model_width),
         EXPERT,
@@ -75,15 +75,22 @@
         tiled=True,
     )
     arrived = arrived.reshape(sources * capacity, model_width)
-    summed = sent_and_summed(
-        lax.dot_general(
-            arrived, cached, (((0,), (0,)), ((), ())), preferred_element_type=jnp.float32
-        ).astype(jnp.bfloat16),
+    partial_value = lax.dot_general(
+        arrived, cached, (((0,), (0,)), ((), ())), preferred_element_type=jnp.float32
+    ).astype(jnp.bfloat16)
+    totals = lax.psum_scatter(
+        jnp.broadcast_to(
+            jnp.pad(expert_sums.reshape(1, 1, 2), ((0, 0), (0, 7), (0, 126))), (replicas, 8, 128)
+        ).reshape(replicas * 8, 128),
         DP,
-        0,
+        scatter_dimension=0,
+        tiled=True,
+    )[0, 0:2]
+    summed = lax.psum_scatter(
+        partial_value.astype(jnp.float32), DP, scatter_dimension=0, tiled=True
     )
     product = summed * norm_scale + own_rows
-    step_size = early_sums[1] / early_sums[0]
+    step_size = totals[1] / totals[0]
     new_solution = solution + step_size * own_rows[None]
     new_residual = residual - step_size * product[None]
     return (new_solution, new_residual)

time: 651 us -> 809 us (1.24)
  waiting for transfers between devices: 196 us -> 467 us
  blocking collectives: 386 us -> 254 us
  between operations: 3.32 us -> 18 us
    unnamed x0 -> x1, blocking collectives: none -> 254 us
    all_to_all x1 -> x0, blocking collectives: 204 us -> none  [local(): lax.all_to_all(outgoing.reshape(experts, capacity, model_width), EXPERT,...]
    psum x1 -> x0, blocking collectives: 182 us -> none  [local(): lax.psum(jnp.stack([local_curvature, jnp.sum(residual_rows * residual_row...]
    unnamed x0 -> x3, waiting for transfers between devices: none -> 150 us
    reduce_scatter x0 -> x1, waiting for transfers between devices: none -> 121 us  [local(): lax.psum_scatter(partial_value.astype(jnp.float32), DP, scatter_dimension...]
  transfers between devices with their start and end apart: 2 -> 4, of which waited for: 1 -> 3; matrix products, arithmetic and copies ran while one was open for 1% -> 2% of each run, Pallas kernels for 0% -> 0%
where the time goes in v3:
time: 809 us; the launch traced here: 808 us
  waiting for transfers between devices  467 us (58%)
  blocking collectives  254 us (31%)
  starting transfers between devices  38.2 us (5%)
  between operations  18 us (2%)
  other arithmetic  12.7 us (2%)
  matrix products  9.57 us (1%)
  local copies, waits for them, and re-layouts  8.98 us (1%)
    unnamed x1, blocking collectives  254 us
    all_to_all x1, waiting for transfers between devices, local(): lax.all_to_all(images, EXPERT, split_axis=0, concat_axis=0, tiled=True)  196 us
    unnamed x3, waiting for transfers between devices  150 us
    reduce_scatter x1, waiting for transfers between devices, local(): lax.psum_scatter(partial_value.astype(jnp.float32), DP, scatter_dimension...  121 us
    all_to_all x1, starting transfers between devices, local(): lax.all_to_all(images, EXPERT, split_axis=0, concat_axis=0, tiled=True)  30.5 us
  transfers between devices with their start and end apart: 4, of which 3 were waited for; matrix products, arithmetic and copies ran while one was open for 2% of the time, Pallas kernels for 0%

profile of v3, /device:TPU:1, one launch (start us, length us, event | category | flops | bytes accessed | tf_op | source)
XLA Modules:
  0.0 807.9 jit_solution(1348086286290896529)
XLA Ops:
  7.2 0.0 copy-start
  7.2 1.1 copy-done
  8.3 5.1 fusion.6
  13.4 0.0 copy-start.4
  13.4 0.0 copy-start.3
  13.4 30.5 %all-to-all-start = ((bf16[64,8,2048]{2,1,0:T(8,128)(2,1)}), bf16[64,8,2048]{2,1,0:T(8,128)(2,1)S(1)}, u32[]{:S(2)}, u32[]{:S(2)}) async-start(bf16[64,8,2048]{2,1,0:T(8,128)(2,1)} %fusion.6), calls=%async_computation | async-start | bytes 4194304 | tf_op jit(solution)/shard_map/all_to_all | solution.py:57
  43.9 0.0 copy-done.4
  43.9 0.1 copy.23
  44.0 0.1 eq.29
  44.1 0.1 eq.25
  44.2 0.1 copy.22
  44.3 0.1 mul.93
  44.4 0.0 copy-done.3
  44.4 0.1 copy.26
  44.4 0.1 copy.21
  44.5 0.1 mul.105
  44.6 0.6 reduce-window.6
  45.2 0.2 slice_reduce_fusion
  45.5 0.1 fusion.28
  45.6 196.0 %all-to-all-done = bf16[64,8,2048]{2,1,0:T(8,128)(2,1)S(1)} async-done(((bf16[64,8,2048]{2,1,0:T(8,128)(2,1)}), bf16[64,8,2048]{2,1,0:T(8,128)(2,1)S(1)}, u32[]{:S(2)}, u32[]{:S(2)}) %all-to-all-start) | async-done | bytes 2097184 | tf_op jit(solution)/shard_map/all_to_all | solution.py:57
  241.6 2.3 gather_fusion
  244.0 2.2 fusion.9
  246.2 3.8 scatter_custom_fusion
  250.0 0.0 copy-start.1
  250.0 7.6 all-to-all-start.1
  257.6 0.0 all-reduce.5.cloned.1.call-start
  257.6 1.3 dynamic-slice.1
  259.6 1.6 fusion.21
  261.2 0.0 copy-done.1
  261.2 0.7 multiply_reduce_fusion
  261.9 0.7 multiply_reduce_fusion.1
  263.8 0.8 maximum_dynamic-update-slice_fusion
  264.7 253.6 %all-reduce.1 = f32[128]{0:T(128)S(1)} all-reduce(f32[128]{0:T(128)S(1)} %maximum_dynamic-update-slice_fusion), channel_id=1, replica_groups=mesh['expert_0'=32,'expert_1'=2,'dp_0'=4,'dp_1'=4] {'expert_0','expert_1'}, use_global_device_ids=true, to_apply=%add.1 | all-reduce | flops 128 | bytes 1024
  518.2 0.1 reshape.103
  518.4 0.6 broadcast_bitcast_fusion
  519.1 0.0 all-reduce.5.cloned.1.call-update
  519.1 0.0 reduce-scatter.2.cloned.1.call-start
  519.1 0.0 all-to-all-done.1
  519.1 4.5 fusion
  523.6 0.0 copy-start.2
  523.6 0.0 reduce-scatter.2.cloned.1.call-update
  523.7 1.3 dynamic-slice.2
  525.6 149.7 %all-reduce.5.cloned.1.call-done = f32[128,128]{1,0:T(8,128)} async-done(((f32[128,128]{1,0:T(8,128)}), f32[128,128]{1,0:T(8,128)}) %all-reduce.5.cloned.1.call-update) | async-done | bytes 65552
  675.4 0.7 constant_dynamic-slice_fusion
  676.1 0.6 fusion.30
  678.0 121.1 %reduce-scatter.2.cloned.1.call-done = f32[128,768]{1,0:T(8,128)} async-done(((f32[2048,768]{1,0:T(8,128)}), f32[128,768]{1,0:T(8,128)}) %reduce-scatter.2.cloned.1.call-update) | async-done | bytes 393232 | tf_op jit(solution)/shard_map/reduce_scatter | solution.py:89
  799.0 0.0 copy-done.2
  799.0 2.0 fusion.24
  (9 shorter events, 0.1 us)
Async XLA Ops:
  7.2 1.1 copy-start
  13.4 30.5 %copy-start.4 = (s32[1,32,8]{1,2,0:T(8,128)S(1)}, s32[1,32,8]{1,2,0:T(8,128)}, u32[]{:S(2)}) copy-start(s32[1,32,8]{1,2,0:T(8,128)} %param.7) | copy-start | bytes 3076
  13.4 31.0 %copy-start.3 = (f32[1,32,8]{1,2,0:T(8,128)S(1)}, f32[1,32,8]{1,2,0:T(8,128)}, u32[]{:S(2)}) copy-start(f32[1,32,8]{1,2,0:T(8,128)} %param.8) | copy-start | bytes 3076
  13.4 228.3 %all-to-all-start = ((bf16[64,8,2048]{2,1,0:T(8,128)(2,1)}), bf16[64,8,2048]{2,1,0:T(8,128)(2,1)S(1)}, u32[]{:S(2)}, u32[]{:S(2)}) async-start(bf16[64,8,2048]{2,1,0:T(8,128)(2,1)} %fusion.6), calls=%async_computation | async-start | bytes 4194304 | tf_op jit(solution)/shard_map/all_to_all | solution.py:57
  250.0 11.2 %copy-start.1 = (f32[1,128,768]{2,1,0:T(8,128)S(1)}, f32[1,128,768]{2,1,0:T(8,128)}, u32[]{:S(2)}) copy-start(f32[1,128,768]{2,1,0:T(8,128)} %param.11) | copy-start | bytes 1179652
  250.0 269.1 %all-to-all-start.1 = ((bf16[64,8,2048]{2,1,0:T(8,128)(2,1)}), bf16[64,8,2048]{2,1,0:T(8,128)(2,1)S(1)}, u32[]{:S(2)}, u32[]{:S(2)}) async-start(bf16[64,8,2048]{2,1,0:T(8,128)(2,1)} %bitcast.79), calls=%async_computation.1 | async-start | bytes 4194304 | tf_op jit(solution)/shard_map/all_to_all | solution.py:70
  257.6 417.8 %all-reduce.5.cloned.1.call-start = ((), (), s32[]{:S(2)}) async-start(), calls=%async_computation.4 | async-start | bytes 131072
  519.1 280.0 %reduce-scatter.2.cloned.1.call-start = ((), (), s32[]{:S(2)}) async-start(), calls=%async_computation.3 | async-start | bytes 6684672 | tf_op jit(solution)/shard_map/reduce_scatter | solution.py:89
  523.6 275.4 %copy-start.2 = (f32[1,128,768]{2,1,0:T(8,128)S(1)}, f32[1,128,768]{2,1,0:T(8,128)}, u32[]{:S(2)}) copy-start(f32[1,128,768]{2,1,0:T(8,128)} %param.10) | copy-start | bytes 1179652
Sparse Core Ops, SparseCore 0:
  519.2 156.1 all-reduce.4
  681.7 117.2 reduce-scatter.1

commit v4 on v2

--- a/solution.py
+++ b/solution.py
@@ -24,6 +24,17 @@
     count = lax.axis_size(axis)
     blocks = lax.all_to_all(split_up(value, dim, count), axis, 0, 0, tiled=True)
     return jnp.sum(blocks.astype(jnp.float32), axis=0)
+
+
+def as_pieces(values):
+    high = lax.reduce_precision(values, exponent_bits=8, mantissa_bits=7)
+    low = (values - high).astype(jnp.bfloat16)
+    return jnp.concatenate([high.astype(jnp.bfloat16), low]).reshape(1, 1, 4)
+
+
+def from_pieces(received):
+    pieces = received.astype(jnp.float32)
+    return jnp.sum(pieces[:, 0:2] + pieces[:, 2:4], axis=0)
 
 
 def slot_numbers(flat_ids, experts):
@@ -65,28 +76,29 @@
     outgoing = outgoing.at[position].set(weighted.reshape(tok_rows * top_count, model_width))
     local_curvature = norm_scale * jnp.sum(tangent * tangent) + jnp.sum(own_rows * own_rows)
     local_sums = jnp.stack([local_curvature, jnp.sum(residual_rows * residual_rows)])
-    sums_high = local_sums.astype(jnp.bfloat16)
-    sums_low = (local_sums - sums_high.astype(jnp.float32)).astype(jnp.bfloat16)
     lanes = 128
-    carried = jnp.zeros((experts, capacity, lanes), jnp.bfloat16)
-    carried = carried.at[:, 0, 0:2].set(sums_high).at[:, 0, 2:4].set(sums_low)
-    payload = jnp.concatenate(
-        [outgoing.reshape(experts, capacity, model_width), carried], axis=2
+    carried = jnp.broadcast_to(
+        jnp.pad(as_pieces(local_sums), ((0, 0), (0, capacity - 1), (0, lanes - 4))),
+        (experts, capacity, lanes),
     )
+    payload = jnp.concatenate([outgoing.reshape(experts, capacity, model_width), carried], axis=2)
     arrived_full = lax.all_to_all(payload, EXPERT, split_axis=0, concat_axis=0, tiled=True)
-    pieces = arrived_full[:, 0, model_width : model_width + 4].astype(jnp.float32)
-    expert_sums = jnp.sum(pieces[:, 0:2] + pieces[:, 2:4], axis=0)
+    expert_sums = from_pieces(arrived_full[:, 0, model_width : model_width + 4])
     arrived = arrived_full[:, :, :model_width].reshape(sources * capacity, model_width)
-    summed = sent_and_summed(
-        lax.dot_general(
-            arrived, cached, (((0,), (0,)), ((), ())), preferred_element_type=jnp.float32
-        ).astype(jnp.bfloat16),
-        DP,
-        0,
+    partial_value = lax.dot_general(
+        arrived, cached, (((0,), (0,)), ((), ())), preferred_element_type=jnp.float32
+    ).astype(jnp.bfloat16)
+    extra_rows = 16
+    extra = jnp.broadcast_to(
+        jnp.pad(as_pieces(expert_sums), ((0, 0), (0, extra_rows - 1), (0, hidden_units - 4))),
+        (replicas, extra_rows, hidden_units),
     )
-    early_sums = lax.psum(expert_sums, DP)
+    blocks = jnp.concatenate([split_up(partial_value, 0, replicas), extra], axis=1)
+    exchanged = lax.all_to_all(blocks, DP, 0, 0, tiled=True)
+    summed = jnp.sum(exchanged[:, :shard_rows].astype(jnp.float32), axis=0)
+    totals = from_pieces(exchanged[:, shard_rows, 0:4])
     product = summed * norm_scale + own_rows
-    step_size = early_sums[1] / early_sums[0]
+    step_size = totals[1] / totals[0]
     new_solution = solution + step_size * own_rows[None]
     new_residual = residual - step_size * product[None]
     return (new_solution, new_residual)

time: 563 us -> 523 us (0.929)
  blocking collectives: 279 us -> 265 us
  local copies, waits for them, and re-layouts: 17.8 us -> 6.85 us
  starting transfers between devices: 37.3 us -> 30.5 us
    psum x1 -> x0, blocking collectives: 61.6 us -> none  [local(): early_sums = lax.psum(expert_sums, DP)]
    all_to_all x0 -> x1, blocking collectives: none -> 47.6 us  [local(): exchanged = lax.all_to_all(blocks, DP, 0, 0, tiled=True)]
    scatter x2 -> x0, local copies, waits for them, and re-layouts: 12.3 us -> none  [local(): carried = carried.at[:, 0, 0:2].set(sums_high).at[:, 0, 2:4].set(sums_low)]
    all_to_all x1 -> x0, starting transfers between devices: 6.8 us -> none  [sent_and_summed(): blocks = lax.all_to_all(split_up(value, dim, count), axis, 0, 0, tiled=True)]
  transfers between devices with their start and end apart: 2 -> 1, of which waited for: 1 -> 1; matrix products, arithmetic and copies ran while one was open for 1% -> 1% of each run, Pallas kernels for 0% -> 0%
where the time goes in v4:
time: 523 us; the launch traced here: 521 us
  blocking collectives  265 us (51%)
  waiting for transfers between devices  194 us (37%)
  starting transfers between devices  30.5 us (6%)
  other arithmetic  14.7 us (3%)
  matrix products  6.92 us (1%)
  local copies, waits for them, and re-layouts  6.85 us (1%)
    all_to_all x1, blocking collectives, local(): lax.all_to_all(payload, EXPERT, split_axis=0, concat_axis=0, tiled=True)  217 us
    all_to_all x1, waiting for transfers between devices, local(): lax.all_to_all(images, EXPERT, split_axis=0, concat_axis=0, tiled=True)  194 us
    all_to_all x1, blocking collectives, local(): exchanged = lax.all_to_all(blocks, DP, 0, 0, tiled=True)  47.6 us
    all_to_all x1, starting transfers between devices, local(): lax.all_to_all(images, EXPERT, split_axis=0, concat_axis=0, tiled=True)  30.5 us
  transfers between devices with their start and end apart: 1, of which 1 were waited for; matrix products, arithmetic and copies ran while one was open for 1% of the time, Pallas kernels for 0%

profile of v4, /device:TPU:1, one launch (start us, length us, event | category | flops | bytes accessed | tf_op | source)
XLA Modules:
  0.0 520.7 jit_solution(12372199269180703402)
XLA Ops:
  0.6 0.0 copy-start
  0.6 1.1 copy-done
  1.8 5.1 fusion.5
  6.8 0.0 copy-start.5
  6.8 0.0 copy-start.4
  6.8 0.0 copy-start.2
  6.8 30.5 %all-to-all-start = ((bf16[64,8,2048]{2,1,0:T(8,128)(2,1)}), bf16[64,8,2048]{2,1,0:T(8,128)(2,1)S(1)}, u32[]{:S(2)}, u32[]{:S(2)}) async-start(bf16[64,8,2048]{2,1,0:T(8,128)(2,1)} %fusion.5), calls=%async_computation | async-start | bytes 4194304 | tf_op jit(solution)/shard_map/all_to_all | solution.py:68
  37.4 0.0 copy-done.5
  37.4 0.1 copy.40
  37.5 0.1 eq.29
  37.6 0.1 eq.25
  37.7 0.1 copy.39
  37.7 0.1 mul.99
  37.8 0.0 copy-done.4
  37.8 0.1 copy.43
  37.9 0.1 copy.44
  38.0 0.1 mul.101
  38.1 0.6 reduce-window.6
  38.7 0.2 slice_reduce_fusion
  38.9 1.7 fusion.17
  40.6 0.1 fusion.23
  40.7 0.0 copy-done.2
  40.7 0.7 multiply_reduce_fusion
  41.4 193.7 %all-to-all-done = bf16[64,8,2048]{2,1,0:T(8,128)(2,1)S(1)} async-done(((bf16[64,8,2048]{2,1,0:T(8,128)(2,1)}), bf16[64,8,2048]{2,1,0:T(8,128)(2,1)S(1)}, u32[]{:S(2)}, u32[]{:S(2)}) %all-to-all-start) | async-done | bytes 2097184 | tf_op jit(solution)/shard_map/all_to_all | solution.py:68
  235.1 2.3 gather_fusion
  237.4 2.2 fusion.8
  239.6 0.7 multiply_reduce_fusion.1
  241.6 0.7 reduce-precision_convert_fusion.1
  242.3 0.1 maximum_bitcast_fusion
  242.4 2.9 scatter_custom_fusion
  245.3 0.2 pad_maximum_fusion.1
  245.5 217.1 %all_to_all.15 = bf16[64,8,2176]{2,1,0:T(8,128)(2,1)S(1)} all-to-all(bf16[64,8,2176]{2,1,0:T(8,128)(2,1)S(1)} %pad_maximum_fusion.1), channel_id=1, replica_groups=mesh['expert_0'=32,'expert_1'=2,'dp_0'=4,'dp_1'=4] {'expert_0','expert_1'}, dimensions={0} | all-to-all | bytes 4456448 | tf_op jit(solution)/shard_map/all_to_all | solution.py:85
  462.6 0.1 fusion.25
  462.7 0.1 maximum_bitcast_fusion.1
  462.8 1.9 convolution_convert_fusion
  464.7 0.2 pad_maximum_fusion
  464.9 47.6 %all_to_all.16 = bf16[16,144,768]{2,1,0:T(8,128)(2,1)S(1)} all-to-all(bf16[16,144,768]{2,1,0:T(8,128)(2,1)S(1)} %pad_maximum_fusion), channel_id=1, replica_groups=mesh['expert_0'=32,'expert_1'=2,'dp_0'=4,'dp_1'=4] {'dp_0','dp_1'}, dimensions={0} | all-to-all | bytes 7077888 | tf_op jit(solution)/shard_map/all_to_all | solution.py:97
  512.5 0.0 copy-start.1
  512.5 1.8 copy-done.1
  514.3 0.0 copy-start.3
  514.3 0.1 copy.48
  514.4 0.1 add_reduce_fusion
  514.5 0.6 fusion.28
  516.4 2.4 convert_reduce_fusion
  518.8 0.0 copy-done.3
  518.8 1.9 fusion.20
  (14 shorter events, 0.2 us)
Async XLA Ops:
  0.6 1.1 copy-start
  6.8 30.6 %copy-start.5 = (s32[1,32,8]{1,2,0:T(8,128)S(1)}, s32[1,32,8]{1,2,0:T(8,128)}, u32[]{:S(2)}) copy-start(s32[1,32,8]{1,2,0:T(8,128)} %param.7) | copy-start | bytes 3076
  6.8 31.0 %copy-start.4 = (f32[1,32,8]{1,2,0:T(8,128)S(1)}, f32[1,32,8]{1,2,0:T(8,128)}, u32[]{:S(2)}) copy-start(f32[1,32,8]{1,2,0:T(8,128)} %param.8) | copy-start | bytes 3076
  6.8 33.9 %copy-start.2 = (f32[1,128,768]{2,1,0:T(8,128)S(1)}, f32[1,128,768]{2,1,0:T(8,128)}, u32[]{:S(2)}) copy-start(f32[1,128,768]{2,1,0:T(8,128)} %param.11) | copy-start | bytes 1179652
  6.8 228.3 %all-to-all-start = ((bf16[64,8,2048]{2,1,0:T(8,128)(2,1)}), bf16[64,8,2048]{2,1,0:T(8,128)(2,1)S(1)}, u32[]{:S(2)}, u32[]{:S(2)}) async-start(bf16[64,8,2048]{2,1,0:T(8,128)(2,1)} %fusion.5), calls=%async_computation | async-start | bytes 4194304 | tf_op jit(solution)/shard_map/all_to_all | solution.py:68
  512.5 1.8 copy-start.1
  514.3 4.5 copy-start.3

commit v5 on v4

--- a/solution.py
+++ b/solution.py
@@ -35,6 +35,24 @@
 def from_pieces(received):
     pieces = received.astype(jnp.float32)
     return jnp.sum(pieces[:, 0:2] + pieces[:, 2:4], axis=0)
+
+
+def dp_sum(blocks, sides):
+    me = lax.axis_index(DP)
+    count = sides[0] * sides[1]
+    total = lax.dynamic_index_in_dim(blocks, me, 0, keepdims=False).astype(jnp.float32)
+    for step in range(1, count):
+        first, second = divmod(step, sides[1])
+        pairs = []
+        for source in range(count):
+            row, col = divmod(source, sides[1])
+            target = ((row + first) % sides[0]) * sides[1] + (col + second) % sides[1]
+            pairs.append((source, target))
+        target_of_me = dict(pairs)
+        goes = jnp.asarray([target_of_me[i] for i in range(count)], jnp.int32)[me]
+        sent = lax.dynamic_index_in_dim(blocks, goes, 0, keepdims=False)
+        total = total + lax.ppermute(sent, DP, pairs).astype(jnp.float32)
+    return total
 
 
 def slot_numbers(flat_ids, experts):
@@ -93,10 +111,16 @@
         jnp.pad(as_pieces(expert_sums), ((0, 0), (0, extra_rows - 1), (0, hidden_units - 4))),
         (replicas, extra_rows, hidden_units),
     )
-    blocks = jnp.concatenate([split_up(partial_value, 0, replicas), extra], axis=1)
+    split_rows = shard_rows // 2
+    grouped = split_up(partial_value, 0, replicas)
+    blocks = jnp.concatenate([grouped[:, split_rows:], extra], axis=1)
     exchanged = lax.all_to_all(blocks, DP, 0, 0, tiled=True)
-    summed = jnp.sum(exchanged[:, :shard_rows].astype(jnp.float32), axis=0)
-    totals = from_pieces(exchanged[:, shard_rows, 0:4])
+    permuted = dp_sum(grouped[:, :split_rows], (lax.axis_size(DP[0]), lax.axis_size(DP[1])))
+    summed = jnp.concatenate(
+        [permuted, jnp.sum(exchanged[:, : shard_rows - split_rows].astype(jnp.float32), axis=0)],
+        axis=0,
+    )
+    totals = from_pieces(exchanged[:, shard_rows - split_rows, 0:4])
     product = summed * norm_scale + own_rows
     step_size = totals[1] / totals[0]
     new_solution = solution + step_size * own_rows[None]

time: 523 us -> 585 us (1.12)
  starting transfers between devices: 30.5 us -> 90.7 us
  blocking collectives: 265 us -> 217 us
  between operations: 3.4 us -> 31.9 us
  local copies, waits for them, and re-layouts: 6.85 us -> 18 us
  waiting for transfers between devices: 194 us -> 200 us
    ppermute x0 -> x15, starting transfers between devices: none -> 53.2 us  [dp_sum(): total = total + lax.ppermute(sent, DP, pairs).astype(jnp.float32)]
    all_to_all x1 -> x0, blocking collectives: 47.6 us -> none  [local(): exchanged = lax.all_to_all(blocks, DP, 0, 0, tiled=True)]
    dynamic_slice x0 -> x15, local copies, waits for them, and re-layouts: none -> 9.23 us  [dp_sum(): goes = jnp.asarray([target_of_me[i] for i in range(count)], jnp.int32)[me]]
    ppermute x0 -> x15, waiting for transfers between devices: none -> 7.14 us  [dp_sum(): total = total + lax.ppermute(sent, DP, pairs).astype(jnp.float32)]
    all_to_all x0 -> x1, starting transfers between devices: none -> 6.9 us  [local(): exchanged = lax.all_to_all(blocks, DP, 0, 0, tiled=True)]
  transfers between devices with their start and end apart: 1 -> 17, of which waited for: 1 -> 3; matrix products, arithmetic and copies ran while one was open for 1% -> 3% of each run, Pallas kernels for 0% -> 0%
where the time goes in v5:
time: 585 us; the launch traced here: 580 us
  blocking collectives  217 us (37%)
  waiting for transfers between devices  200 us (34%)
  starting transfers between devices  90.7 us (16%)
  between operations  31.9 us (5%)
  local copies, waits for them, and re-layouts  18 us (3%)
  other arithmetic  15.3 us (3%)
  matrix products  6.91 us (1%)
    all_to_all x1, blocking collectives, local(): lax.all_to_all(payload, EXPERT, split_axis=0, concat_axis=0, tiled=True)  217 us
    all_to_all x1, waiting for transfers between devices, local(): lax.all_to_all(images, EXPERT, split_axis=0, concat_axis=0, tiled=True)  193 us
    ppermute x15, starting transfers between devices, dp_sum(): total = total + lax.ppermute(sent, DP, pairs).astype(jnp.float32)  53.2 us
    all_to_all x1, starting transfers between devices, local(): lax.all_to_all(images, EXPERT, split_axis=0, concat_axis=0, tiled=True)  30.5 us
  transfers between devices with their start and end apart: 17, of which 3 were waited for; matrix products, arithmetic and copies ran while one was open for 3% of the time, Pallas kernels for 0%

profile of v5, /device:TPU:1, one launch (start us, length us, event | category | flops | bytes accessed | tf_op | source)
XLA Modules:
  0.0 579.9 jit_solution(342993867309953904)
XLA Ops:
  0.6 1.1 copy-done
  1.8 5.0 fusion.5
  6.8 30.5 %all-to-all-start = ((bf16[64,8,2048]{2,1,0:T(8,128)(2,1)}), bf16[64,8,2048]{2,1,0:T(8,128)(2,1)S(1)}, u32[]{:S(2)}, u32[]{:S(2)}) async-start(bf16[64,8,2048]{2,1,0:T(8,128)(2,1)} %fusion.5), calls=%async_computation | async-start | bytes 4194304 | tf_op jit(solution)/shard_map/all_to_all | solution.py:86
  37.7 0.6 reduce-window.6
  38.8 0.7 mul.99
  39.5 1.7 fusion.17
  41.3 0.8 multiply_reduce_fusion
  42.1 193.0 %all-to-all-done = bf16[64,8,2048]{2,1,0:T(8,128)(2,1)S(1)} async-done(((bf16[64,8,2048]{2,1,0:T(8,128)(2,1)}), bf16[64,8,2048]{2,1,0:T(8,128)(2,1)S(1)}, u32[]{:S(2)}, u32[]{:S(2)}) %all-to-all-start) | async-done | bytes 2097184 | tf_op jit(solution)/shard_map/all_to_all | solution.py:86
  235.1 2.3 gather_fusion
  237.4 2.2 fusion.8
  239.6 0.7 multiply_reduce_fusion.1
  241.6 0.7 reduce-precision_convert_fusion.1
  242.5 3.0 scatter_custom_fusion
  245.7 217.1 %all_to_all.15 = bf16[64,8,2176]{2,1,0:T(8,128)(2,1)S(1)} all-to-all(bf16[64,8,2176]{2,1,0:T(8,128)(2,1)S(1)} %pad_maximum_fusion), channel_id=1, replica_groups=mesh['expert_0'=32,'expert_1'=2,'dp_0'=4,'dp_1'=4] {'expert_0','expert_1'}, dimensions={0} | all-to-all | bytes 4456448 | tf_op jit(solution)/shard_map/all_to_all | solution.py:103
  463.0 1.9 convolution_convert_fusion
  464.8 1.4 fusion.43
  466.3 1.4 pad_maximum_fusion.1
  467.9 6.9 %all-to-all-start.2 = ((bf16[16,80,768]{2,1,0:T(8,128)(2,1)}), bf16[16,80,768]{2,1,0:T(8,128)(2,1)S(1)}, u32[]{:S(2)}, u32[]{:S(2)}) async-start(bf16[16,80,768]{2,1,0:T(8,128)(2,1)} %pad_maximum_fusion.1), calls=%async_computation.2 | async-start | bytes 3932160 | tf_op jit(solution)/shard_map/all_to_all | solution.py:117
  476.7 0.7 dynamic_slice.101
  478.7 0.7 dynamic_slice.103
  482.3 0.6 dynamic_slice.107
  484.2 0.6 dynamic_slice.109
  486.0 0.7 dynamic_slice.111
  488.0 0.6 dynamic_slice.113
  489.9 0.6 dynamic_slice.115
  495.2 0.7 dynamic_slice.121
  497.2 0.7 dynamic_slice.123
  499.2 0.6 dynamic_slice.125
  512.2 1.6 dynamic-slice_bitcast_fusion.14
  513.8 3.3 collective-permute-start
  517.0 4.3 collective-permute-start.1
  521.4 5.5 collective-permute-start.10
  526.9 2.8 collective-permute-start.11
  529.7 1.9 collective-permute-start.12
  531.6 3.7 collective-permute-start.13
  535.3 4.3 collective-permute-start.14
  539.6 3.1 collective-permute-start.2
  542.7 2.2 collective-permute-start.3
  544.9 2.5 collective-permute-start.4
  547.5 5.2 collective-permute-start.5
  552.6 4.0 collective-permute-start.6
  556.7 2.8 collective-permute-start.7
  559.5 4.6 collective-permute-start.8
  564.1 3.1 collective-permute-start.9
  567.2 1.2 collective-permute-done.8
  568.5 5.9 %collective-permute-done.9 = bf16[64,768]{1,0:T(8,128)(2,1)S(1)} collective-permute-done((bf16[64,768]{1,0:T(8,128)(2,1)S(1)}, bf16[64,768]{1,0:T(8,128)(2,1)S(1)}, u32[]{:S(2)}, u32[]{:S(2)}) %collective-permute-start.9) | collective-permute-done | bytes 98336 | tf_op jit(solution)/shard_map/ppermute | solution.py:54
  574.4 1.1 fusion.35
  577.8 2.1 fusion.20
  (89 shorter events, 5.5 us)
Async XLA Ops:
  0.6 1.1 copy-start
  6.8 30.6 %copy-start.3 = (s32[1,32,8]{1,2,0:T(8,128)S(1)}, s32[1,32,8]{1,2,0:T(8,128)}, u32[]{:S(2)}) copy-start(s32[1,32,8]{1,2,0:T(8,128)} %param.22) | copy-start | bytes 3076
  6.8 31.9 %copy-start.2 = (f32[1,32,8]{1,2,0:T(8,128)S(1)}, f32[1,32,8]{1,2,0:T(8,128)}, u32[]{:S(2)}) copy-start(f32[1,32,8]{1,2,0:T(8,128)} %param.23) | copy-start | bytes 3076
  6.8 34.5 %copy-start.1 = (f32[1,128,768]{2,1,0:T(8,128)S(1)}, f32[1,128,768]{2,1,0:T(8,128)}, u32[]{:S(2)}) copy-start(f32[1,128,768]{2,1,0:T(8,128)} %param.26) | copy-start | bytes 1179652
  6.8 228.3 %all-to-all-start = ((bf16[64,8,2048]{2,1,0:T(8,128)(2,1)}), bf16[64,8,2048]{2,1,0:T(8,128)(2,1)S(1)}, u32[]{:S(2)}, u32[]{:S(2)}) async-start(bf16[64,8,2048]{2,1,0:T(8,128)(2,1)} %fusion.5), calls=%async_computation | async-start | bytes 4194304 | tf_op jit(solution)/shard_map/all_to_all | solution.py:86
  41.3 193.8 %copy-start.4 = (s32[256,1]{0,1:T(1,128)}, s32[256,1]{0,1:T(1,128)S(1)}, u32[]{:S(2)}) copy-start(s32[256,1]{0,1:T(1,128)S(1)} %compare_select_fusion) | copy-start | bytes 3076
  467.7 7.1 %copy-start.19 = (s32[16]{0:T(128)S(1)}, s32[16]{0:T(128)}, u32[]{:S(2)}) copy-start(s32[16]{0:T(128)} %constant.99.clone) | copy-start | bytes 196
  467.7 9.0 %copy-start.18 = (s32[16]{0:T(128)S(1)}, s32[16]{0:T(128)}, u32[]{:S(2)}) copy-start(s32[16]{0:T(128)} %constant.100.clone) | copy-start | bytes 196
  467.7 11.0 %copy-start.17 = (s32[16]{0:T(128)S(1)}, s32[16]{0:T(128)}, u32[]{:S(2)}) copy-start(s32[16]{0:T(128)} %constant.101.clone) | copy-start | bytes 196
  467.7 12.9 %copy-start.16 = (s32[16]{0:T(128)S(1)}, s32[16]{0:T(128)}, u32[]{:S(2)}) copy-start(s32[16]{0:T(128)} %constant.102.clone) | copy-start | bytes 196
  467.8 14.6 %copy-start.15 = (s32[16]{0:T(128)S(1)}, s32[16]{0:T(128)}, u32[]{:S(2)}) copy-start(s32[16]{0:T(128)} %constant.103.clone) | copy-start | bytes 196
  467.8 16.4 %copy-start.14 = (s32[16]{0:T(128)S(1)}, s32[16]{0:T(128)}, u32[]{:S(2)}) copy-start(s32[16]{0:T(128)} %constant.104.clone) | copy-start | bytes 196
  467.8 18.2 %copy-start.13 = (s32[16]{0:T(128)S(1)}, s32[16]{0:T(128)}, u32[]{:S(2)}) copy-start(s32[16]{0:T(128)} %constant.105.clone) | copy-start | bytes 196
  467.8 20.2 %copy-start.12 = (s32[16]{0:T(128)S(1)}, s32[16]{0:T(128)}, u32[]{:S(2)}) copy-start(s32[16]{0:T(128)} %constant.106.clone) | copy-start | bytes 196
  467.8 22.1 %copy-start.11 = (s32[16]{0:T(128)S(1)}, s32[16]{0:T(128)}, u32[]{:S(2)}) copy-start(s32[16]{0:T(128)} %constant.107.clone) | copy-start | bytes 196
  467.8 23.9 %copy-start.10 = (s32[16]{0:T(128)S(1)}, s32[16]{0:T(128)}, u32[]{:S(2)}) copy-start(s32[16]{0:T(128)} %constant.108.clone) | copy-start | bytes 196
  467.8 25.7 %copy-start.9 = (s32[16]{0:T(128)S(1)}, s32[16]{0:T(128)}, u32[]{:S(2)}) copy-start(s32[16]{0:T(128)} %constant.109.clone) | copy-start | bytes 196
  467.8 27.3 %copy-start.8 = (s32[16]{0:T(128)S(1)}, s32[16]{0:T(128)}, u32[]{:S(2)}) copy-start(s32[16]{0:T(128)} %constant.110.clone) | copy-start | bytes 196
  467.9 29.4 %copy-start.7 = (s32[16]{0:T(128)S(1)}, s32[16]{0:T(128)}, u32[]{:S(2)}) copy-start(s32[16]{0:T(128)} %constant.111.clone) | copy-start | bytes 196
  467.9 31.3 %copy-start.6 = (s32[16]{0:T(128)S(1)}, s32[16]{0:T(128)}, u32[]{:S(2)}) copy-start(s32[16]{0:T(128)} %constant.112.clone) | copy-start | bytes 196
  467.9 33.1 %copy-start.5 = (s32[16]{0:T(128)S(1)}, s32[16]{0:T(128)}, u32[]{:S(2)}) copy-start(s32[16]{0:T(128)} %constant.113.clone) | copy-start | bytes 196
  467.9 107.6 %all-to-all-start.2 = ((bf16[16,80,768]{2,1,0:T(8,128)(2,1)}), bf16[16,80,768]{2,1,0:T(8,128)(2,1)S(1)}, u32[]{:S(2)}, u32[]{:S(2)}) async-start(bf16[16,80,768]{2,1,0:T(8,128)(2,1)} %pad_maximum_fusion.1), calls=%async_computation.2 | async-start | bytes 3932160 | tf_op jit(solution)/shard_map/all_to_all | solution.py:117
  513.8 17.8 %collective-permute-start = (bf16[64,768]{1,0:T(8,128)(2,1)S(1)}, bf16[64,768]{1,0:T(8,128)(2,1)S(1)}, u32[]{:S(2)}, u32[]{:S(2)}) collective-permute-start(bf16[64,768]{1,0:T(8,128)(2,1)S(1)} %get-tuple-element.6), channel_id=1, source_target_pairs={{0,1},{1,2},{2,3},{3,0},{4,5},{5,6},{6,7},{7,4},{8,9},{9,10},{10,1... | collective-permute-start | bytes 294920 | tf_op jit(solution)/shard_map/ppermute | solution.py:54
  517.0 18.2 %collective-permute-start.1 = (bf16[64,768]{1,0:T(8,128)(2,1)S(1)}, bf16[64,768]{1,0:T(8,128)(2,1)S(1)}, u32[]{:S(2)}, u32[]{:S(2)}) collective-permute-start(bf16[64,768]{1,0:T(8,128)(2,1)S(1)} %get-tuple-element.20), channel_id=1, source_target_pairs={{0,2},{1,3},{2,0},{3,1},{4,6},{5,7},{6,4},{7,5},{8,10},{9,11},{10,... | collective-permute-start | bytes 294920 | tf_op jit(solution)/shard_map/ppermute | solution.py:54
  521.4 18.2 %collective-permute-start.10 = (bf16[64,768]{1,0:T(8,128)(2,1)S(1)}, bf16[64,768]{1,0:T(8,128)(2,1)S(1)}, u32[]{:S(2)}, u32[]{:S(2)}) collective-permute-start(bf16[64,768]{1,0:T(8,128)(2,1)S(1)} %get-tuple-element.11), channel_id=1, source_target_pairs={{0,11},{1,8},{2,9},{3,10},{4,15},{5,12},{6,13},{7,14},{8,3},{9,0},... | collective-permute-start | bytes 294920 | tf_op jit(solution)/shard_map/ppermute | solution.py:54
  526.9 15.8 %collective-permute-start.11 = (bf16[64,768]{1,0:T(8,128)(2,1)S(1)}, bf16[64,768]{1,0:T(8,128)(2,1)S(1)}, u32[]{:S(2)}, u32[]{:S(2)}) collective-permute-start(bf16[64,768]{1,0:T(8,128)(2,1)S(1)} %get-tuple-element.10), channel_id=1, source_target_pairs={{0,12},{1,13},{2,14},{3,15},{4,0},{5,1},{6,2},{7,3},{8,4},{9,5},{1... | collective-permute-start | bytes 294920 | tf_op jit(solution)/shard_map/ppermute | solution.py:54
  529.7 15.2 %collective-permute-start.12 = (bf16[64,768]{1,0:T(8,128)(2,1)S(1)}, bf16[64,768]{1,0:T(8,128)(2,1)S(1)}, u32[]{:S(2)}, u32[]{:S(2)}) collective-permute-start(bf16[64,768]{1,0:T(8,128)(2,1)S(1)} %get-tuple-element.9), channel_id=1, source_target_pairs={{0,13},{1,14},{2,15},{3,12},{4,1},{5,2},{6,3},{7,0},{8,5},{9,6},{1... | collective-permute-start | bytes 294920 | tf_op jit(solution)/shard_map/ppermute | solution.py:54
  531.6 15.8 %collective-permute-start.13 = (bf16[64,768]{1,0:T(8,128)(2,1)S(1)}, bf16[64,768]{1,0:T(8,128)(2,1)S(1)}, u32[]{:S(2)}, u32[]{:S(2)}) collective-permute-start(bf16[64,768]{1,0:T(8,128)(2,1)S(1)} %get-tuple-element.8), channel_id=1, source_target_pairs={{0,14},{1,15},{2,12},{3,13},{4,2},{5,3},{6,0},{7,1},{8,6},{9,7},{1... | collective-permute-start | bytes 294920 | tf_op jit(solution)/shard_map/ppermute | solution.py:54
  535.3 17.4 %collective-permute-start.14 = (bf16[64,768]{1,0:T(8,128)(2,1)S(1)}, bf16[64,768]{1,0:T(8,128)(2,1)S(1)}, u32[]{:S(2)}, u32[]{:S(2)}) collective-permute-start(bf16[64,768]{1,0:T(8,128)(2,1)S(1)} %get-tuple-element.7), channel_id=1, source_target_pairs={{0,15},{1,12},{2,13},{3,14},{4,3},{5,0},{6,1},{7,2},{8,7},{9,4},{1... | collective-permute-start | bytes 294920 | tf_op jit(solution)/shard_map/ppermute | solution.py:54
  539.6 17.1 %collective-permute-start.2 = (bf16[64,768]{1,0:T(8,128)(2,1)S(1)}, bf16[64,768]{1,0:T(8,128)(2,1)S(1)}, u32[]{:S(2)}, u32[]{:S(2)}) collective-permute-start(bf16[64,768]{1,0:T(8,128)(2,1)S(1)} %get-tuple-element.19), channel_id=1, source_target_pairs={{0,3},{1,0},{2,1},{3,2},{4,7},{5,4},{6,5},{7,6},{8,11},{9,8},{10,9... | collective-permute-start | bytes 294920 | tf_op jit(solution)/shard_map/ppermute | solution.py:54
  542.7 16.8 %collective-permute-start.3 = (bf16[64,768]{1,0:T(8,128)(2,1)S(1)}, bf16[64,768]{1,0:T(8,128)(2,1)S(1)}, u32[]{:S(2)}, u32[]{:S(2)}) collective-permute-start(bf16[64,768]{1,0:T(8,128)(2,1)S(1)} %get-tuple-element.18), channel_id=1, source_target_pairs={{0,4},{1,5},{2,6},{3,7},{4,8},{5,9},{6,10},{7,11},{8,12},{9,13},{1... | collective-permute-start | bytes 294920 | tf_op jit(solution)/shard_map/ppermute | solution.py:54
  544.9 19.1 %collective-permute-start.4 = (bf16[64,768]{1,0:T(8,128)(2,1)S(1)}, bf16[64,768]{1,0:T(8,128)(2,1)S(1)}, u32[]{:S(2)}, u32[]{:S(2)}) collective-permute-start(bf16[64,768]{1,0:T(8,128)(2,1)S(1)} %get-tuple-element.17), channel_id=1, source_target_pairs={{0,5},{1,6},{2,7},{3,4},{4,9},{5,10},{6,11},{7,8},{8,13},{9,14},{1... | collective-permute-start | bytes 294920 | tf_op jit(solution)/shard_map/ppermute | solution.py:54
  547.5 19.8 %collective-permute-start.5 = (bf16[64,768]{1,0:T(8,128)(2,1)S(1)}, bf16[64,768]{1,0:T(8,128)(2,1)S(1)}, u32[]{:S(2)}, u32[]{:S(2)}) collective-permute-start(bf16[64,768]{1,0:T(8,128)(2,1)S(1)} %get-tuple-element.16), channel_id=1, source_target_pairs={{0,6},{1,7},{2,4},{3,5},{4,10},{5,11},{6,8},{7,9},{8,14},{9,15},{1... | collective-permute-start | bytes 294920 | tf_op jit(solution)/shard_map/ppermute | solution.py:54
  552.6 14.6 %collective-permute-start.6 = (bf16[64,768]{1,0:T(8,128)(2,1)S(1)}, bf16[64,768]{1,0:T(8,128)(2,1)S(1)}, u32[]{:S(2)}, u32[]{:S(2)}) collective-permute-start(bf16[64,768]{1,0:T(8,128)(2,1)S(1)} %get-tuple-element.15), channel_id=1, source_target_pairs={{0,7},{1,4},{2,5},{3,6},{4,11},{5,8},{6,9},{7,10},{8,15},{9,12},{1... | collective-permute-start | bytes 294920 | tf_op jit(solution)/shard_map/ppermute | solution.py:54
  556.7 10.6 %collective-permute-start.7 = (bf16[64,768]{1,0:T(8,128)(2,1)S(1)}, bf16[64,768]{1,0:T(8,128)(2,1)S(1)}, u32[]{:S(2)}, u32[]{:S(2)}) collective-permute-start(bf16[64,768]{1,0:T(8,128)(2,1)S(1)} %get-tuple-element.14), channel_id=1, source_target_pairs={{0,8},{1,9},{2,10},{3,11},{4,12},{5,13},{6,14},{7,15},{8,0},{9,1},... | collective-permute-start | bytes 294920 | tf_op jit(solution)/shard_map/ppermute | solution.py:54
  559.5 9.0 %collective-permute-start.8 = (bf16[64,768]{1,0:T(8,128)(2,1)S(1)}, bf16[64,768]{1,0:T(8,128)(2,1)S(1)}, u32[]{:S(2)}, u32[]{:S(2)}) collective-permute-start(bf16[64,768]{1,0:T(8,128)(2,1)S(1)} %get-tuple-element.13), channel_id=1, source_target_pairs={{0,9},{1,10},{2,11},{3,8},{4,13},{5,14},{6,15},{7,12},{8,1},{9,2},... | collective-permute-start | bytes 294920 | tf_op jit(solution)/shard_map/ppermute | solution.py:54
  564.1 10.3 %collective-permute-start.9 = (bf16[64,768]{1,0:T(8,128)(2,1)S(1)}, bf16[64,768]{1,0:T(8,128)(2,1)S(1)}, u32[]{:S(2)}, u32[]{:S(2)}) collective-permute-start(bf16[64,768]{1,0:T(8,128)(2,1)S(1)} %get-tuple-element.12), channel_id=1, source_target_pairs={{0,10},{1,11},{2,8},{3,9},{4,14},{5,15},{6,12},{7,13},{8,2},{9,3},... | collective-permute-start | bytes 294920 | tf_op jit(solution)/shard_map/ppermute | solution.py:54

commit v6 on v4

--- a/solution.py
+++ b/solution.py
@@ -88,7 +88,7 @@
     partial_value = lax.dot_general(
         arrived, cached, (((0,), (0,)), ((), ())), preferred_element_type=jnp.float32
     ).astype(jnp.bfloat16)
-    extra_rows = 16
+    extra_rows = 8
     extra = jnp.broadcast_to(
         jnp.pad(as_pieces(expert_sums), ((0, 0), (0, extra_rows - 1), (0, hidden_units - 4))),
         (replicas, extra_rows, hidden_units),

time: 523 us -> 520 us (level)
  no operation moved by 1% of the time
where the time goes in v6:
time: 520 us; the launch traced here: 519 us
  blocking collectives  263 us (51%)
  waiting for transfers between devices  194 us (37%)
  starting transfers between devices  30.5 us (6%)
  other arithmetic  14.7 us (3%)
  matrix products  6.92 us (1%)
  local copies, waits for them, and re-layouts  6.76 us (1%)
    all_to_all x1, blocking collectives, local(): lax.all_to_all(payload, EXPERT, split_axis=0, concat_axis=0, tiled=True)  217 us
    all_to_all x1, waiting for transfers between devices, local(): lax.all_to_all(images, EXPERT, split_axis=0, concat_axis=0, tiled=True)  194 us
    all_to_all x1, blocking collectives, local(): exchanged = lax.all_to_all(blocks, DP, 0, 0, tiled=True)  45.9 us
    all_to_all x1, starting transfers between devices, local(): lax.all_to_all(images, EXPERT, split_axis=0, concat_axis=0, tiled=True)  30.5 us
  transfers between devices with their start and end apart: 1, of which 1 were waited for; matrix products, arithmetic and copies ran while one was open for 1% of the time, Pallas kernels for 0%

profile of v6, /device:TPU:1, one launch (start us, length us, event | category | flops | bytes accessed | tf_op | source)
XLA Modules:
  0.0 519.0 jit_solution(769375096114853931)
XLA Ops:
  0.6 0.0 copy-start
  0.6 1.1 copy-done
  1.8 5.1 fusion.5
  6.8 0.0 copy-start.5
  6.8 0.0 copy-start.4
  6.8 0.0 copy-start.2
  6.8 30.5 %all-to-all-start = ((bf16[64,8,2048]{2,1,0:T(8,128)(2,1)}), bf16[64,8,2048]{2,1,0:T(8,128)(2,1)S(1)}, u32[]{:S(2)}, u32[]{:S(2)}) async-start(bf16[64,8,2048]{2,1,0:T(8,128)(2,1)} %fusion.5), calls=%async_computation | async-start | bytes 4194304 | tf_op jit(solution)/shard_map/all_to_all | solution.py:68
  37.4 0.0 copy-done.5
  37.4 0.1 copy.40
  37.5 0.1 eq.29
  37.6 0.1 eq.25
  37.7 0.1 copy.39
  37.7 0.1 mul.99
  37.8 0.0 copy-done.4
  37.8 0.1 copy.43
  37.9 0.1 copy.44
  38.0 0.1 mul.101
  38.1 0.6 reduce-window.6
  38.7 0.2 slice_reduce_fusion
  38.9 1.7 fusion.17
  40.6 0.1 fusion.23
  40.7 0.0 copy-done.2
  40.7 0.7 multiply_reduce_fusion
  41.4 193.7 %all-to-all-done = bf16[64,8,2048]{2,1,0:T(8,128)(2,1)S(1)} async-done(((bf16[64,8,2048]{2,1,0:T(8,128)(2,1)}), bf16[64,8,2048]{2,1,0:T(8,128)(2,1)S(1)}, u32[]{:S(2)}, u32[]{:S(2)}) %all-to-all-start) | async-done | bytes 2097184 | tf_op jit(solution)/shard_map/all_to_all | solution.py:68
  235.1 2.3 gather_fusion
  237.4 2.2 fusion.8
  239.6 0.7 multiply_reduce_fusion.1
  241.6 0.7 reduce-precision_convert_fusion.1
  242.3 0.1 maximum_bitcast_fusion
  242.4 2.9 scatter_custom_fusion
  245.3 0.2 pad_maximum_fusion.1
  245.5 217.1 %all_to_all.15 = bf16[64,8,2176]{2,1,0:T(8,128)(2,1)S(1)} all-to-all(bf16[64,8,2176]{2,1,0:T(8,128)(2,1)S(1)} %pad_maximum_fusion.1), channel_id=1, replica_groups=mesh['expert_0'=32,'expert_1'=2,'dp_0'=4,'dp_1'=4] {'expert_0','expert_1'}, dimensions={0} | all-to-all | bytes 4456448 | tf_op jit(solution)/shard_map/all_to_all | solution.py:85
  462.6 0.1 fusion.25
  462.7 0.1 maximum_bitcast_fusion.1
  462.8 1.9 convolution_convert_fusion
  464.7 0.2 pad_maximum_fusion
  464.9 45.9 %all_to_all.16 = bf16[16,136,768]{2,1,0:T(8,128)(2,1)S(1)} all-to-all(bf16[16,136,768]{2,1,0:T(8,128)(2,1)S(1)} %pad_maximum_fusion), channel_id=1, replica_groups=mesh['expert_0'=32,'expert_1'=2,'dp_0'=4,'dp_1'=4] {'dp_0','dp_1'}, dimensions={0} | all-to-all | bytes 6684672 | tf_op jit(solution)/shard_map/all_to_all | solution.py:97
  510.8 0.0 copy-start.1
  510.8 1.7 copy-done.1
  512.5 0.0 copy-start.3
  512.5 0.1 copy.48
  512.6 0.1 add_reduce_fusion
  512.7 0.6 fusion.28
  514.7 2.4 convert_reduce_fusion
  517.0 0.0 copy-done.3
  517.1 1.9 fusion.20
  (14 shorter events, 0.2 us)
Async XLA Ops:
  0.6 1.1 copy-start
  6.8 30.6 %copy-start.5 = (s32[1,32,8]{1,2,0:T(8,128)S(1)}, s32[1,32,8]{1,2,0:T(8,128)}, u32[]{:S(2)}) copy-start(s32[1,32,8]{1,2,0:T(8,128)} %param.7) | copy-start | bytes 3076
  6.8 31.0 %copy-start.4 = (f32[1,32,8]{1,2,0:T(8,128)S(1)}, f32[1,32,8]{1,2,0:T(8,128)}, u32[]{:S(2)}) copy-start(f32[1,32,8]{1,2,0:T(8,128)} %param.8) | copy-start | bytes 3076
  6.8 33.9 %copy-start.2 = (f32[1,128,768]{2,1,0:T(8,128)S(1)}, f32[1,128,768]{2,1,0:T(8,128)}, u32[]{:S(2)}) copy-start(f32[1,128,768]{2,1,0:T(8,128)} %param.11) | copy-start | bytes 1179652
  6.8 228.3 %all-to-all-start = ((bf16[64,8,2048]{2,1,0:T(8,128)(2,1)}), bf16[64,8,2048]{2,1,0:T(8,128)(2,1)S(1)}, u32[]{:S(2)}, u32[]{:S(2)}) async-start(bf16[64,8,2048]{2,1,0:T(8,128)(2,1)} %fusion.5), calls=%async_computation | async-start | bytes 4194304 | tf_op jit(solution)/shard_map/all_to_all | solution.py:68
  510.8 1.7 copy-start.1
  512.5 4.5 copy-start.3

commit v7 on v6

--- a/solution.py
+++ b/solution.py
@@ -81,10 +81,26 @@
         jnp.pad(as_pieces(local_sums), ((0, 0), (0, capacity - 1), (0, lanes - 4))),
         (experts, capacity, lanes),
     )
-    payload = jnp.concatenate([outgoing.reshape(experts, capacity, model_width), carried], axis=2)
+    halves = 2
+    half_rows = shard_rows // halves
+    width = replicas * half_rows
+    split_out = outgoing.reshape(experts, capacity, replicas, halves, half_rows)
+    first = split_out[:, :, :, 0].reshape(experts, capacity, width)
+    second = split_out[:, :, :, 1].reshape(experts, capacity, width)
+    arrived_first = lax.all_to_all(first, EXPERT, split_axis=0, concat_axis=0, tiled=True)
+    partial_first = lax.dot_general(
+        arrived_first.reshape(sources * capacity, width),
+        cached,
+        (((0,), (0,)), ((), ())),
+        preferred_element_type=jnp.float32,
+    ).astype(jnp.bfloat16)
+    summed_first = lax.psum_scatter(
+        partial_first.astype(jnp.float32), DP, scatter_dimension=0, tiled=True
+    )
+    payload = jnp.concatenate([second, carried], axis=2)
     arrived_full = lax.all_to_all(payload, EXPERT, split_axis=0, concat_axis=0, tiled=True)
-    expert_sums = from_pieces(arrived_full[:, 0, model_width : model_width + 4])
-    arrived = arrived_full[:, :, :model_width].reshape(sources * capacity, model_width)
+    expert_sums = from_pieces(arrived_full[:, 0, width : width + 4])
+    arrived = arrived_full[:, :, :width].reshape(sources * capacity, width)
     partial_value = lax.dot_general(
         arrived, cached, (((0,), (0,)), ((), ())), preferred_element_type=jnp.float32
     ).astype(jnp.bfloat16)
@@ -95,8 +111,9 @@
     )
     blocks = jnp.concatenate([split_up(partial_value, 0, replicas), extra], axis=1)
     exchanged = lax.all_to_all(blocks, DP, 0, 0, tiled=True)
-    summed = jnp.sum(exchanged[:, :shard_rows].astype(jnp.float32), axis=0)
-    totals = from_pieces(exchanged[:, shard_rows, 0:4])
+    summed_second = jnp.sum(exchanged[:, :half_rows].astype(jnp.float32), axis=0)
+    totals = from_pieces(exchanged[:, half_rows, 0:4])
+    summed = jnp.stack([summed_first, summed_second], axis=0).reshape(shard_rows, hidden_units)
     product = summed * norm_scale + own_rows
     step_size = totals[1] / totals[0]
     new_solution = solution + step_size * own_rows[None]

time: 520 us -> 573 us (1.10)
  blocking collectives: 263 us -> 27.5 us
  waiting for transfers between devices: 194 us -> 410 us
  local copies, waits for them, and re-layouts: 6.76 us -> 44.2 us
  starting transfers between devices: 30.5 us -> 46.1 us
  between operations: 3.4 us -> 16.8 us
    all_to_all x1 -> x0, blocking collectives: 217 us -> none  [local(): lax.all_to_all(payload, EXPERT, split_axis=0, concat_axis=0, tiled=True)]
    all_to_all x0 -> x2, waiting for transfers between devices: none -> 214 us  [the longest x1 115 us: local(): lax.all_to_all(payload, EXPERT, split_axis=0, concat_axis=0, tiled=True)]
    slice x2 -> x3, local copies, waits for them, and re-layouts: 0.19 us -> 27.6 us  [the longest x1 27.4 us: local(): first = split_out[:, :, :, 0].reshape(experts, capacity, width)]
    all_to_all x1, blocking collectives: 45.9 us -> 27.5 us  [local(): exchanged = lax.all_to_all(blocks, DP, 0, 0, tiled=True)]
    all_to_all x0 -> x2, starting transfers between devices: none -> 15.5 us  [the longest x1 8.19 us: local(): lax.all_to_all(first, EXPERT, split_axis=0, concat_axis=0, tiled=True)]
    another operation x1 -> x3, local copies, waits for them, and re-layouts: 0.01 us -> 6.42 us  [the longest x1 4.15 us: local(): first = split_out[:, :, :, 0].reshape(experts, capacity, width)]
  transfers between devices with their start and end apart: 1 -> 4, of which waited for: 1 -> 3; matrix products, arithmetic and copies ran while one was open for 1% -> 3% of each run, Pallas kernels for 0% -> 0%
where the time goes in v7:
time: 573 us; the launch traced here: 570 us
  waiting for transfers between devices  410 us (72%)
  starting transfers between devices  46.1 us (8%)
  local copies, waits for them, and re-layouts  44.2 us (8%)
  blocking collectives  27.5 us (5%)
  between operations  16.8 us (3%)
  other arithmetic  15.7 us (3%)
  matrix products  9.99 us (2%)
    all_to_all x1, waiting for transfers between devices, local(): lax.all_to_all(images, EXPERT, split_axis=0, concat_axis=0, tiled=True)  196 us
    all_to_all x1, waiting for transfers between devices, local(): lax.all_to_all(payload, EXPERT, split_axis=0, concat_axis=0, tiled=True)  115 us
    all_to_all x1, waiting for transfers between devices, local(): lax.all_to_all(first, EXPERT, split_axis=0, concat_axis=0, tiled=True)  98.2 us
    all_to_all x1, starting transfers between devices, local(): lax.all_to_all(images, EXPERT, split_axis=0, concat_axis=0, tiled=True)  30.5 us
    all_to_all x1, blocking collectives, local(): exchanged = lax.all_to_all(blocks, DP, 0, 0, tiled=True)  27.5 us
    slice x1, local copies, waits for them, and re-layouts, local(): first = split_out[:, :, :, 0].reshape(experts, capacity, width)  27.4 us
  transfers between devices with their start and end apart: 4, of which 3 were waited for; matrix products, arithmetic and copies ran while one was open for 3% of the time, Pallas kernels for 0%

profile of v7, /device:TPU:1, one launch (start us, length us, event | category | flops | bytes accessed | tf_op | source)
XLA Modules:
  0.0 570.0 jit_solution(10976426077583775075)
XLA Ops:
  7.2 0.0 copy-start
  7.2 1.1 copy-done
  8.3 5.1 fusion.5
  13.4 30.5 %all-to-all-start = ((bf16[64,8,2048]{2,1,0:T(8,128)(2,1)}), bf16[64,8,2048]{2,1,0:T(8,128)(2,1)S(1)}, u32[]{:S(2)}, u32[]{:S(2)}) async-start(bf16[64,8,2048]{2,1,0:T(8,128)(2,1)} %fusion.5), calls=%async_computation | async-start | bytes 4194304 | tf_op jit(solution)/shard_map/all_to_all | solution.py:68
  43.9 0.1 copy.32
  44.0 0.1 eq.29
  44.1 0.1 eq.25
  44.2 0.1 copy.31
  44.3 0.1 mul.99
  44.4 0.1 copy.35
  44.4 0.1 copy.36
  44.5 0.1 mul.101
  44.6 0.6 reduce-window.6
  45.2 0.2 slice_reduce_fusion.2
  45.5 0.1 fusion.26
  45.6 196.0 %all-to-all-done = bf16[64,8,2048]{2,1,0:T(8,128)(2,1)S(1)} async-done(((bf16[64,8,2048]{2,1,0:T(8,128)(2,1)}), bf16[64,8,2048]{2,1,0:T(8,128)(2,1)S(1)}, u32[]{:S(2)}, u32[]{:S(2)}) %all-to-all-start) | async-done | bytes 2097184 | tf_op jit(solution)/shard_map/all_to_all | solution.py:68
  241.6 2.3 gather_fusion
  244.0 2.2 fusion.8
  246.2 3.1 scatter_custom_fusion
  249.3 5.3 reshape.119
  254.6 27.4 %slice_reduce_fusion = (bf16[64,8,16,64]{3,2,1,0:T(8,128)(2,1)}, bf16[64,8,16,64]{3,2,1,0:T(8,128)(2,1)S(1)}) fusion(bf16[64,8,16,2,64]{4,3,2,1,0:T(2,128)(2,1)} %reshape.119), kind=kLoop, calls=%fused_computation.2 | loop fusion | bytes 4194304 | tf_op jit(solution)/shard_map/slice | solution.py:88
  282.0 4.1 reshape_squeeze.7
  286.2 8.2 %all-to-all-start.3 = ((bf16[64,8,1024]{2,1,0:T(8,128)(2,1)}), bf16[64,8,1024]{2,1,0:T(8,128)(2,1)}, u32[]{:S(2)}, u32[]{:S(2)}) async-start(bf16[64,8,1024]{2,1,0:T(8,128)(2,1)} %reshape_squeeze.7), calls=%async_computation.3 | async-start | bytes 2097152 | tf_op jit(solution)/shard_map/all_to_all | solution.py:90
  294.4 1.6 fusion.20
  296.0 0.7 multiply_reduce_fusion
  296.7 2.3 reshape_squeeze.6
  299.0 0.7 multiply_reduce_fusion.1
  300.9 0.7 reduce-precision_convert_fusion.1
  301.6 0.1 maximum_bitcast_fusion
  301.7 2.3 pad_maximum_fusion.1
  304.1 98.2 %all-to-all-done.3 = bf16[64,8,1024]{2,1,0:T(8,128)(2,1)} async-done(((bf16[64,8,1024]{2,1,0:T(8,128)(2,1)}), bf16[64,8,1024]{2,1,0:T(8,128)(2,1)}, u32[]{:S(2)}, u32[]{:S(2)}) %all-to-all-start.3) | async-done | bytes 1048608 | tf_op jit(solution)/shard_map/all_to_all | solution.py:90
  402.3 7.3 %all-to-all-start.1 = ((bf16[64,8,1152]{2,1,0:T(8,128)(2,1)}), bf16[64,8,1152]{2,1,0:T(8,128)(2,1)S(1)}, u32[]{:S(2)}, u32[]{:S(2)}) async-start(bf16[64,8,1152]{2,1,0:T(8,128)(2,1)} %pad_maximum_fusion.1), calls=%async_computation.1 | async-start | bytes 2359296 | tf_op jit(solution)/shard_map/all_to_all | solution.py:101
  409.7 0.0 reduce-scatter.2.cloned.1.call-start
  409.7 3.9 fusion.10
  413.6 0.0 reduce-scatter.2.cloned.1.call-update
  413.6 115.4 %all-to-all-done.1 = bf16[64,8,1152]{2,1,0:T(8,128)(2,1)S(1)} async-done(((bf16[64,8,1152]{2,1,0:T(8,128)(2,1)}), bf16[64,8,1152]{2,1,0:T(8,128)(2,1)S(1)}, u32[]{:S(2)}, u32[]{:S(2)}) %all-to-all-start.1) | async-done | bytes 1179680 | tf_op jit(solution)/shard_map/all_to_all | solution.py:101
  529.0 0.1 fusion.28
  529.1 0.1 maximum_bitcast_fusion.1
  529.2 1.0 convolution_convert_fusion.1
  530.2 0.1 pad_maximum_fusion
  530.4 27.5 %all_to_all.20 = bf16[16,72,768]{2,1,0:T(8,128)(2,1)S(1)} all-to-all(bf16[16,72,768]{2,1,0:T(8,128)(2,1)S(1)} %pad_maximum_fusion), channel_id=1, replica_groups=mesh['expert_0'=32,'expert_1'=2,'dp_0'=4,'dp_1'=4] {'dp_0','dp_1'}, dimensions={0} | all-to-all | bytes 3538944 | tf_op jit(solution)/shard_map/all_to_all | solution.py:113
  557.9 0.1 copy.38
  558.0 0.1 add_reduce_fusion
  558.1 0.6 fusion.31
  560.0 0.2 convert_reduce_fusion
  560.2 0.0 reduce-scatter.2.cloned.1.call-done
  560.3 1.0 maximum_multiply_fusion
  561.2 1.9 fusion.23
  (22 shorter events, 0.2 us)
Async XLA Ops:
  7.2 1.1 copy-start
  13.4 30.6 %copy-start.4 = (s32[1,32,8]{1,2,0:T(8,128)S(1)}, s32[1,32,8]{1,2,0:T(8,128)}, u32[]{:S(2)}) copy-start(s32[1,32,8]{1,2,0:T(8,128)} %param.7) | copy-start | bytes 3076
  13.4 31.0 %copy-start.3 = (f32[1,32,8]{1,2,0:T(8,128)S(1)}, f32[1,32,8]{1,2,0:T(8,128)}, u32[]{:S(2)}) copy-start(f32[1,32,8]{1,2,0:T(8,128)} %param.8) | copy-start | bytes 3076
  13.4 228.3 %all-to-all-start = ((bf16[64,8,2048]{2,1,0:T(8,128)(2,1)}), bf16[64,8,2048]{2,1,0:T(8,128)(2,1)S(1)}, u32[]{:S(2)}, u32[]{:S(2)}) async-start(bf16[64,8,2048]{2,1,0:T(8,128)(2,1)} %fusion.5), calls=%async_computation | async-start | bytes 4194304 | tf_op jit(solution)/shard_map/all_to_all | solution.py:68
  282.0 14.0 %copy-start.1 = (f32[1,128,768]{2,1,0:T(8,128)S(1)}, f32[1,128,768]{2,1,0:T(8,128)}, u32[]{:S(2)}) copy-start(f32[1,128,768]{2,1,0:T(8,128)} %param.11) | copy-start | bytes 1179652
  286.2 116.2 %all-to-all-start.3 = ((bf16[64,8,1024]{2,1,0:T(8,128)(2,1)}), bf16[64,8,1024]{2,1,0:T(8,128)(2,1)}, u32[]{:S(2)}, u32[]{:S(2)}) async-start(bf16[64,8,1024]{2,1,0:T(8,128)(2,1)} %reshape_squeeze.7), calls=%async_computation.3 | async-start | bytes 2097152 | tf_op jit(solution)/shard_map/all_to_all | solution.py:90
  402.3 126.7 %all-to-all-start.1 = ((bf16[64,8,1152]{2,1,0:T(8,128)(2,1)}), bf16[64,8,1152]{2,1,0:T(8,128)(2,1)S(1)}, u32[]{:S(2)}, u32[]{:S(2)}) async-start(bf16[64,8,1152]{2,1,0:T(8,128)(2,1)} %pad_maximum_fusion.1), calls=%async_computation.1 | async-start | bytes 2359296 | tf_op jit(solution)/shard_map/all_to_all | solution.py:101
  409.7 150.6 %reduce-scatter.2.cloned.1.call-start = ((), (), s32[]{:S(2)}) async-start(), calls=%async_computation.5 | async-start | bytes 3342336 | tf_op jit(solution)/shard_map/reduce_scatter | solution.py:97
  557.8 3.4 copy-start.2
Sparse Core Ops, SparseCore 0:
  415.9 110.3 reduce-scatter.1

commit v8 on v6

--- a/solution.py
+++ b/solution.py
@@ -66,14 +66,26 @@
     )
     images = images.astype(jnp.bfloat16).reshape(sources, capacity, model_width)
     returned = lax.all_to_all(images, EXPERT, split_axis=0, concat_axis=0, tiled=True)
-    row_images = returned.reshape(experts * capacity, model_width)[position]
+    selector = (
+        position[:, None] == jnp.arange(experts * capacity, dtype=jnp.int32)[None, :]
+    ).astype(jnp.bfloat16)
+    row_images = lax.dot_general(
+        selector,
+        returned.reshape(experts * capacity, model_width),
+        (((1,), (0,)), ((), ())),
+        preferred_element_type=jnp.float32,
+    )
     gate_rows = gate_weights.reshape(tok_rows, top_count)
     tangent = jnp.sum(
         gate_rows[:, :, None] * row_images.reshape(tok_rows, top_count, model_width), axis=1
     )
     weighted = (gate_rows[:, :, None] * tangent[:, None, :]).astype(jnp.bfloat16)
-    outgoing = jnp.zeros((experts * capacity, model_width), jnp.bfloat16)
-    outgoing = outgoing.at[position].set(weighted.reshape(tok_rows * top_count, model_width))
+    outgoing = lax.dot_general(
+        selector,
+        weighted.reshape(tok_rows * top_count, model_width),
+        (((0,), (0,)), ((), ())),
+        preferred_element_type=jnp.float32,
+    ).astype(jnp.bfloat16)
     local_curvature = norm_scale * jnp.sum(tangent * tangent) + jnp.sum(own_rows * own_rows)
     local_sums = jnp.stack([local_curvature, jnp.sum(residual_rows * residual_rows)])
     lanes = 128

time: 520 us -> 516 us (level)
  no operation moved by 1% of the time
where the time goes in v8:
time: 516 us; the launch traced here: 515 us
  blocking collectives  263 us (51%)
  waiting for transfers between devices  192 us (37%)
  starting transfers between devices  30.5 us (6%)
  matrix products  10.2 us (2%)
  other arithmetic  10.2 us (2%)
  local copies, waits for them, and re-layouts  5.5 us (1%)
    all_to_all x1, blocking collectives, local(): lax.all_to_all(payload, EXPERT, split_axis=0, concat_axis=0, tiled=True)  217 us
    all_to_all x1, waiting for transfers between devices, local(): lax.all_to_all(images, EXPERT, split_axis=0, concat_axis=0, tiled=True)  192 us
    all_to_all x1, blocking collectives, local(): exchanged = lax.all_to_all(blocks, DP, 0, 0, tiled=True)  45.9 us
    all_to_all x1, starting transfers between devices, local(): lax.all_to_all(images, EXPERT, split_axis=0, concat_axis=0, tiled=True)  30.5 us
  transfers between devices with their start and end apart: 1, of which 1 were waited for; matrix products, arithmetic and copies ran while one was open for 1% of the time, Pallas kernels for 0%

profile of v8, /device:TPU:1, one launch (start us, length us, event | category | flops | bytes accessed | tf_op | source)
XLA Modules:
  0.0 514.8 jit_solution(6053081349555815364)
XLA Ops:
  0.6 0.0 copy-start
  0.6 1.1 copy-done
  1.8 5.1 fusion.6
  6.8 0.0 copy-start.5
  6.8 0.0 copy-start.4
  6.8 0.0 copy-start.2
  6.8 30.5 %all-to-all-start = ((bf16[64,8,2048]{2,1,0:T(8,128)(2,1)}), bf16[64,8,2048]{2,1,0:T(8,128)(2,1)S(1)}, u32[]{:S(2)}, u32[]{:S(2)}) async-start(bf16[64,8,2048]{2,1,0:T(8,128)(2,1)} %fusion.6), calls=%async_computation | async-start | bytes 4194304 | tf_op jit(solution)/shard_map/all_to_all | solution.py:68
  37.4 0.0 copy-done.5
  37.4 0.1 copy.32
  37.5 0.1 reshape.114
  37.6 0.1 eq.61
  37.7 0.0 copy-done.4
  37.7 0.1 copy.35
  37.7 0.7 copy.36
  38.4 0.7 mul.102
  39.1 0.6 reduce-window.6
  39.7 0.2 slice_reduce_fusion
  39.9 0.1 fusion.29
  40.0 0.1 reduce_sum.75
  40.1 1.7 fusion.21
  41.8 0.0 copy-done.2
  41.8 0.7 multiply_reduce_fusion
  42.5 0.6 multiply_add_fusion
  43.1 192.0 %all-to-all-done = bf16[64,8,2048]{2,1,0:T(8,128)(2,1)S(1)} async-done(((bf16[64,8,2048]{2,1,0:T(8,128)(2,1)}), bf16[64,8,2048]{2,1,0:T(8,128)(2,1)S(1)}, u32[]{:S(2)}, u32[]{:S(2)}) %all-to-all-start) | async-done | bytes 2097184 | tf_op jit(solution)/shard_map/all_to_all | solution.py:68
  235.1 1.7 fusion.11
  236.8 0.7 multiply_reduce_fusion.1
  238.8 0.7 reduce-precision_convert_fusion.1
  239.5 0.1 maximum_bitcast_fusion
  239.5 1.5 fusion.5
  241.1 0.2 pad_maximum_fusion.1
  241.3 217.1 %all_to_all.15 = bf16[64,8,2176]{2,1,0:T(8,128)(2,1)S(1)} all-to-all(bf16[64,8,2176]{2,1,0:T(8,128)(2,1)S(1)} %pad_maximum_fusion.1), channel_id=1, replica_groups=mesh['expert_0'=32,'expert_1'=2,'dp_0'=4,'dp_1'=4] {'expert_0','expert_1'}, dimensions={0} | all-to-all | bytes 4456448 | tf_op jit(solution)/shard_map/all_to_all | solution.py:97
  458.4 0.1 fusion.31
  458.5 0.1 maximum_bitcast_fusion.1
  458.6 1.9 convolution_convert_fusion
  460.5 0.2 pad_maximum_fusion
  460.7 45.9 %all_to_all.16 = bf16[16,136,768]{2,1,0:T(8,128)(2,1)S(1)} all-to-all(bf16[16,136,768]{2,1,0:T(8,128)(2,1)S(1)} %pad_maximum_fusion), channel_id=1, replica_groups=mesh['expert_0'=32,'expert_1'=2,'dp_0'=4,'dp_1'=4] {'dp_0','dp_1'}, dimensions={0} | all-to-all | bytes 6684672 | tf_op jit(solution)/shard_map/all_to_all | solution.py:109
  506.6 0.0 copy-start.1
  506.6 1.7 copy-done.1
  508.3 0.0 copy-start.3
  508.3 0.1 copy.39
  508.4 0.1 add_reduce_fusion
  508.5 0.6 fusion.34
  510.5 2.4 convert_reduce_fusion
  512.8 0.0 copy-done.3
  512.9 1.9 fusion.24
  (12 shorter events, 0.1 us)
Async XLA Ops:
  0.6 1.1 copy-start
  6.8 30.6 %copy-start.5 = (s32[1,32,8]{1,2,0:T(8,128)S(1)}, s32[1,32,8]{1,2,0:T(8,128)}, u32[]{:S(2)}) copy-start(s32[1,32,8]{1,2,0:T(8,128)} %param.7) | copy-start | bytes 3076
  6.8 30.8 %copy-start.4 = (f32[1,32,8]{1,2,0:T(8,128)S(1)}, f32[1,32,8]{1,2,0:T(8,128)}, u32[]{:S(2)}) copy-start(f32[1,32,8]{1,2,0:T(8,128)} %param.8) | copy-start | bytes 3076
  6.8 34.9 %copy-start.2 = (f32[1,128,768]{2,1,0:T(8,128)S(1)}, f32[1,128,768]{2,1,0:T(8,128)}, u32[]{:S(2)}) copy-start(f32[1,128,768]{2,1,0:T(8,128)} %param.11) | copy-start | bytes 1179652
  6.8 228.3 %all-to-all-start = ((bf16[64,8,2048]{2,1,0:T(8,128)(2,1)}), bf16[64,8,2048]{2,1,0:T(8,128)(2,1)S(1)}, u32[]{:S(2)}, u32[]{:S(2)}) async-start(bf16[64,8,2048]{2,1,0:T(8,128)(2,1)} %fusion.6), calls=%async_computation | async-start | bytes 4194304 | tf_op jit(solution)/shard_map/all_to_all | solution.py:68
  506.6 1.7 copy-start.1
  508.3 4.5 copy-start.3

commit v9 on v8

--- a/solution.py
+++ b/solution.py
@@ -107,7 +107,9 @@
     )
     blocks = jnp.concatenate([split_up(partial_value, 0, replicas), extra], axis=1)
     exchanged = lax.all_to_all(blocks, DP, 0, 0, tiled=True)
-    summed = jnp.sum(exchanged[:, :shard_rows].astype(jnp.float32), axis=0)
+    summed = functools.reduce(
+        jnp.add, [exchanged[i, :shard_rows].astype(jnp.float32) for i in range(replicas)]
+    )
     totals = from_pieces(exchanged[:, shard_rows, 0:4])
     product = summed * norm_scale + own_rows
     step_size = totals[1] / totals[0]

time: 516 us -> 517 us (level)
  no operation moved by 1% of the time
where the time goes in v9:
time: 517 us; the launch traced here: 516 us
  blocking collectives  263 us (51%)
  waiting for transfers between devices  192 us (37%)
  starting transfers between devices  30.5 us (6%)
  other arithmetic  10.9 us (2%)
  matrix products  10.2 us (2%)
  local copies, waits for them, and re-layouts  5.5 us (1%)
    all_to_all x1, blocking collectives, local(): lax.all_to_all(payload, EXPERT, split_axis=0, concat_axis=0, tiled=True)  217 us
    all_to_all x1, waiting for transfers between devices, local(): lax.all_to_all(images, EXPERT, split_axis=0, concat_axis=0, tiled=True)  192 us
    all_to_all x1, blocking collectives, local(): exchanged = lax.all_to_all(blocks, DP, 0, 0, tiled=True)  46.1 us
    all_to_all x1, starting transfers between devices, local(): lax.all_to_all(images, EXPERT, split_axis=0, concat_axis=0, tiled=True)  30.5 us
  transfers between devices with their start and end apart: 1, of which 1 were waited for; matrix products, arithmetic and copies ran while one was open for 1% of the time, Pallas kernels for 0%

profile of v9, /device:TPU:1, one launch (start us, length us, event | category | flops | bytes accessed | tf_op | source)
XLA Modules:
  0.0 515.5 jit_solution(2187825830467246333)
XLA Ops:
  0.6 0.0 copy-start
  0.6 1.1 copy-done
  1.8 5.1 fusion.6
  6.8 0.0 copy-start.5
  6.8 0.0 copy-start.4
  6.8 0.0 copy-start.2
  6.8 30.5 %all-to-all-start = ((bf16[64,8,2048]{2,1,0:T(8,128)(2,1)}), bf16[64,8,2048]{2,1,0:T(8,128)(2,1)S(1)}, u32[]{:S(2)}, u32[]{:S(2)}) async-start(bf16[64,8,2048]{2,1,0:T(8,128)(2,1)} %fusion.6), calls=%async_computation | async-start | bytes 4194304 | tf_op jit(solution)/shard_map/all_to_all | solution.py:68
  37.4 0.0 copy-done.5
  37.4 0.1 copy.48
  37.5 0.1 reshape.105
  37.6 0.1 eq.61
  37.7 0.0 copy-done.4
  37.7 0.1 copy.51
  37.7 0.7 copy.52
  38.4 0.7 mul.93
  39.1 0.6 reduce-window.6
  39.7 0.2 slice_reduce_fusion
  39.9 0.1 fusion.29
  40.0 0.1 reduce_sum.66
  40.1 1.7 fusion.21
  41.8 0.0 copy-done.2
  41.8 0.7 multiply_reduce_fusion
  42.5 0.6 multiply_add_fusion
  43.1 192.0 %all-to-all-done = bf16[64,8,2048]{2,1,0:T(8,128)(2,1)S(1)} async-done(((bf16[64,8,2048]{2,1,0:T(8,128)(2,1)}), bf16[64,8,2048]{2,1,0:T(8,128)(2,1)S(1)}, u32[]{:S(2)}, u32[]{:S(2)}) %all-to-all-start) | async-done | bytes 2097184 | tf_op jit(solution)/shard_map/all_to_all | solution.py:68
  235.1 1.7 fusion.11
  236.8 0.7 multiply_reduce_fusion.1
  238.8 0.7 reduce-precision_convert_fusion.1
  239.5 0.1 maximum_bitcast_fusion
  239.5 1.5 fusion.5
  241.1 0.2 pad_maximum_fusion.1
  241.3 217.1 %all_to_all.15 = bf16[64,8,2176]{2,1,0:T(8,128)(2,1)S(1)} all-to-all(bf16[64,8,2176]{2,1,0:T(8,128)(2,1)S(1)} %pad_maximum_fusion.1), channel_id=1, replica_groups=mesh['expert_0'=32,'expert_1'=2,'dp_0'=4,'dp_1'=4] {'expert_0','expert_1'}, dimensions={0} | all-to-all | bytes 4456448 | tf_op jit(solution)/shard_map/all_to_all | solution.py:97
  458.4 0.1 fusion.31
  458.5 0.1 maximum_bitcast_fusion.1
  458.6 1.9 convolution_convert_fusion
  460.5 0.2 pad_maximum_fusion
  460.7 0.0 copy-start.3
  460.7 46.1 %all_to_all.16 = bf16[16,136,768]{2,1,0:T(8,128)(2,1)S(1)} all-to-all(bf16[16,136,768]{2,1,0:T(8,128)(2,1)S(1)} %pad_maximum_fusion), channel_id=1, replica_groups=mesh['expert_0'=32,'expert_1'=2,'dp_0'=4,'dp_1'=4] {'dp_0','dp_1'}, dimensions={0} | all-to-all | bytes 6684672 | tf_op jit(solution)/shard_map/all_to_all | solution.py:109
  506.8 0.0 copy-start.1
  506.8 1.7 copy-done.1
  508.5 0.1 copy.55
  508.6 0.1 add_reduce_fusion
  508.7 0.6 fusion.34
  510.6 0.0 copy-done.3
  510.6 1.7 fusion.22
  512.3 3.2 fusion.24
  (12 shorter events, 0.1 us)
Async XLA Ops:
  0.6 1.1 copy-start
  6.8 30.6 %copy-start.5 = (s32[1,32,8]{1,2,0:T(8,128)S(1)}, s32[1,32,8]{1,2,0:T(8,128)}, u32[]{:S(2)}) copy-start(s32[1,32,8]{1,2,0:T(8,128)} %param.7) | copy-start | bytes 3076
  6.8 30.8 %copy-start.4 = (f32[1,32,8]{1,2,0:T(8,128)S(1)}, f32[1,32,8]{1,2,0:T(8,128)}, u32[]{:S(2)}) copy-start(f32[1,32,8]{1,2,0:T(8,128)} %param.8) | copy-start | bytes 3076
  6.8 34.9 %copy-start.2 = (f32[1,128,768]{2,1,0:T(8,128)S(1)}, f32[1,128,768]{2,1,0:T(8,128)}, u32[]{:S(2)}) copy-start(f32[1,128,768]{2,1,0:T(8,128)} %param.11) | copy-start | bytes 1179652
  6.8 228.3 %all-to-all-start = ((bf16[64,8,2048]{2,1,0:T(8,128)(2,1)}), bf16[64,8,2048]{2,1,0:T(8,128)(2,1)S(1)}, u32[]{:S(2)}, u32[]{:S(2)}) async-start(bf16[64,8,2048]{2,1,0:T(8,128)(2,1)} %fusion.6), calls=%async_computation | async-start | bytes 4194304 | tf_op jit(solution)/shard_map/all_to_all | solution.py:68
  460.7 49.9 %copy-start.3 = (f32[1,128,768]{2,1,0:T(8,128)S(1)}, f32[1,128,768]{2,1,0:T(8,128)}, u32[]{:S(2)}) copy-start(f32[1,128,768]{2,1,0:T(8,128)} %param.10) | copy-start | bytes 1179652
  506.8 1.7 copy-start.1

commit v10 on v8

--- a/solution.py
+++ b/solution.py
@@ -80,25 +80,37 @@
         gate_rows[:, :, None] * row_images.reshape(tok_rows, top_count, model_width), axis=1
     )
     weighted = (gate_rows[:, :, None] * tangent[:, None, :]).astype(jnp.bfloat16)
-    outgoing = lax.dot_general(
-        selector,
-        weighted.reshape(tok_rows * top_count, model_width),
-        (((0,), (0,)), ((), ())),
-        preferred_element_type=jnp.float32,
-    ).astype(jnp.bfloat16)
+    pairs = capacity // 2
+    slot_rows = jnp.arange(experts * pairs, dtype=jnp.int32)
+    packed = []
+    for parity in range(2):
+        target = (slot_rows // pairs) * capacity + (slot_rows % pairs) * 2 + parity
+        pick = (position[:, None] == target[None, :]).astype(jnp.bfloat16)
+        packed.append(
+            lax.dot_general(
+                pick,
+                weighted.reshape(tok_rows * top_count, model_width),
+                (((0,), (0,)), ((), ())),
+                preferred_element_type=jnp.float32,
+            ).astype(jnp.bfloat16)
+        )
+    outgoing = jnp.concatenate(packed, axis=1).reshape(experts, pairs, 2 * model_width)
     local_curvature = norm_scale * jnp.sum(tangent * tangent) + jnp.sum(own_rows * own_rows)
     local_sums = jnp.stack([local_curvature, jnp.sum(residual_rows * residual_rows)])
     lanes = 128
     carried = jnp.broadcast_to(
-        jnp.pad(as_pieces(local_sums), ((0, 0), (0, capacity - 1), (0, lanes - 4))),
-        (experts, capacity, lanes),
+        jnp.pad(as_pieces(local_sums), ((0, 0), (0, pairs - 1), (0, lanes - 4))),
+        (experts, pairs, lanes),
     )
-    payload = jnp.concatenate([outgoing.reshape(experts, capacity, model_width), carried], axis=2)
+    payload = jnp.concatenate([outgoing, carried], axis=2)
     arrived_full = lax.all_to_all(payload, EXPERT, split_axis=0, concat_axis=0, tiled=True)
-    expert_sums = from_pieces(arrived_full[:, 0, model_width : model_width + 4])
-    arrived = arrived_full[:, :, :model_width].reshape(sources * capacity, model_width)
+    expert_sums = from_pieces(arrived_full[:, 0, 2 * model_width : 2 * model_width + 4])
+    arrived = arrived_full[:, :, : 2 * model_width].reshape(sources, pairs, 2, model_width)
     partial_value = lax.dot_general(
-        arrived, cached, (((0,), (0,)), ((), ())), preferred_element_type=jnp.float32
+        arrived,
+        hidden.reshape(sources, pairs, 2, hidden_units),
+        (((0, 1, 2), (0, 1, 2)), ((), ())),
+        preferred_element_type=jnp.float32,
     ).astype(jnp.bfloat16)
     extra_rows = 8
     extra = jnp.broadcast_to(

time: 516 us -> 520 us (level)
  blocking collectives: 263 us -> 43.3 us
  waiting for transfers between devices: 192 us -> 395 us
  starting transfers between devices: 30.5 us -> 38.1 us
  local copies, waits for them, and re-layouts: 5.5 us -> 12.6 us
    all_to_all x1 -> x0, blocking collectives: 217 us -> none  [local(): lax.all_to_all(payload, EXPERT, split_axis=0, concat_axis=0, tiled=True)]
    all_to_all x0 -> x1, waiting for transfers between devices: none -> 202 us  [local(): lax.all_to_all(payload, EXPERT, split_axis=0, concat_axis=0, tiled=True)]
    reshape x0 -> x3, local copies, waits for them, and re-layouts: none -> 8.62 us  [the longest x1 4.87 us: local(): arrived_full[:, :, :2 * model_width].reshape(sources, pairs, 2, model_width)]
    all_to_all x0 -> x1, starting transfers between devices: none -> 7.58 us  [local(): lax.all_to_all(payload, EXPERT, split_axis=0, concat_axis=0, tiled=True)]
  transfers between devices with their start and end apart: 1 -> 2, of which waited for: 1 -> 2; matrix products, arithmetic and copies ran while one was open for 1% -> 1% of each run, Pallas kernels for 0% -> 0%
where the time goes in v10:
time: 520 us; the launch traced here: 516 us
  waiting for transfers between devices  395 us (76%)
  blocking collectives  43.3 us (8%)
  starting transfers between devices  38.1 us (7%)
  local copies, waits for them, and re-layouts  12.6 us (2%)
  other arithmetic  11.6 us (2%)
  matrix products  11.4 us (2%)
    all_to_all x1, waiting for transfers between devices, local(): lax.all_to_all(payload, EXPERT, split_axis=0, concat_axis=0, tiled=True)  202 us
    all_to_all x1, waiting for transfers between devices, local(): lax.all_to_all(images, EXPERT, split_axis=0, concat_axis=0, tiled=True)  194 us
    all_to_all x1, blocking collectives, local(): exchanged = lax.all_to_all(blocks, DP, 0, 0, tiled=True)  43.3 us
    all_to_all x1, starting transfers between devices, local(): lax.all_to_all(images, EXPERT, split_axis=0, concat_axis=0, tiled=True)  30.5 us
  transfers between devices with their start and end apart: 2, of which 2 were waited for; matrix products, arithmetic and copies ran while one was open for 1% of the time, Pallas kernels for 0%

profile of v10, /device:TPU:1, one launch (start us, length us, event | category | flops | bytes accessed | tf_op | source)
XLA Modules:
  0.0 515.7 jit_solution(5737727722987533060)
XLA Ops:
  0.6 5.3 %fusion.5 = bf16[64,8,2048]{2,1,0:T(8,128)(2,1)} fusion(bf16[1,2048,768]{2,1,0:T(8,128)(2,1)} %param.9, bf16[1,1,64,8,768]{4,3,2,1,0:T(8,128)(2,1)} %param.6), kind=kOutput, calls=%fused_computation.6 | convolution fusion | flops 1611661312 | bytes 6029312 | tf_op jit(solution)/shard_map/dot_general | solution.py:64
  5.9 0.0 copy-start.6
  6.0 0.0 copy-start.5
  6.0 30.5 %all-to-all-start = ((bf16[64,8,2048]{2,1,0:T(8,128)(2,1)}), bf16[64,8,2048]{2,1,0:T(8,128)(2,1)S(1)}, u32[]{:S(2)}, u32[]{:S(2)}) async-start(bf16[64,8,2048]{2,1,0:T(8,128)(2,1)} %fusion.5), calls=%async_computation | async-start | bytes 4194304 | tf_op jit(solution)/shard_map/all_to_all | solution.py:68
  36.5 0.0 copy-done.6
  36.5 0.1 copy.42
  36.6 0.1 reshape.144
  36.7 0.1 eq.82
  36.8 0.0 copy-done.5
  36.8 0.1 copy.45
  36.9 0.1 copy.46
  36.9 0.1 mul.124
  37.0 0.6 reduce-window.6
  37.6 0.2 slice_reduce_fusion
  37.9 0.1 fusion.36
  38.0 0.1 reduce_sum.75
  38.1 1.7 fusion.23
  39.7 0.0 copy-done
  39.7 0.7 multiply_reduce_fusion
  40.4 193.8 %all-to-all-done = bf16[64,8,2048]{2,1,0:T(8,128)(2,1)S(1)} async-done(((bf16[64,8,2048]{2,1,0:T(8,128)(2,1)}), bf16[64,8,2048]{2,1,0:T(8,128)(2,1)S(1)}, u32[]{:S(2)}, u32[]{:S(2)}) %all-to-all-start) | async-done | bytes 2097184 | tf_op jit(solution)/shard_map/all_to_all | solution.py:68
  234.2 1.0 fusion.13
  235.2 0.7 multiply_reduce_fusion.1
  237.2 0.7 reduce-precision_convert_fusion.1
  237.9 0.1 maximum_bitcast_fusion
  238.0 0.6 convolution_convert_fusion
  238.6 0.6 convolution_convert_fusion.1
  239.1 1.6 pad_maximum_fusion.2
  240.7 2.7 reshape.150
  243.5 2.4 pad_maximum_fusion.1
  245.9 7.6 %all-to-all-start.1 = ((bf16[64,4,4224]{2,1,0:T(4,128)(2,1)}), bf16[64,4,4224]{2,1,0:T(4,128)(2,1)S(1)}, u32[]{:S(2)}, u32[]{:S(2)}) async-start(bf16[64,4,4224]{2,1,0:T(4,128)(2,1)} %pad_maximum_fusion.1), calls=%async_computation.1 | async-start | bytes 4325376 | tf_op jit(solution)/shard_map/all_to_all | solution.py:106
  253.5 0.0 copy-done.2
  253.5 1.0 copy.55
  254.5 201.6 %all-to-all-done.1 = bf16[64,4,4224]{2,1,0:T(4,128)(2,1)S(1)} async-done(((bf16[64,4,4224]{2,1,0:T(4,128)(2,1)}), bf16[64,4,4224]{2,1,0:T(4,128)(2,1)S(1)}, u32[]{:S(2)}, u32[]{:S(2)}) %all-to-all-start.1) | async-done | bytes 2162720 | tf_op jit(solution)/shard_map/all_to_all | solution.py:106
  456.1 2.5 slice.49
  458.6 4.9 reshape.160
  463.5 0.1 fusion.38
  463.6 0.1 maximum_bitcast_fusion.1
  463.7 0.0 copy-done.3
  463.7 4.0 bitcast_convert_fusion
  467.7 0.2 pad_maximum_fusion
  467.9 43.3 %all_to_all.15 = bf16[16,136,768]{2,1,0:T(8,128)(2,1)S(1)} all-to-all(bf16[16,136,768]{2,1,0:T(8,128)(2,1)S(1)} %pad_maximum_fusion), channel_id=1, replica_groups=mesh['expert_0'=32,'expert_1'=2,'dp_0'=4,'dp_1'=4] {'dp_0','dp_1'}, dimensions={0} | all-to-all | bytes 6684672 | tf_op jit(solution)/shard_map/all_to_all | solution.py:121
  511.2 0.1 copy.56
  511.3 0.1 add_reduce_fusion
  511.4 0.6 fusion.46
  513.3 0.5 convert_reduce_fusion
  513.8 0.0 copy-done.1
  513.8 0.0 copy-done.4
  513.8 1.9 fusion.26
  (19 shorter events, 0.2 us)
Async XLA Ops:
  5.9 30.6 %copy-start.6 = (s32[1,32,8]{1,2,0:T(8,128)S(1)}, s32[1,32,8]{1,2,0:T(8,128)}, u32[]{:S(2)}) copy-start(s32[1,32,8]{1,2,0:T(8,128)} %param.7) | copy-start | bytes 3076
  6.0 30.8 %copy-start.5 = (f32[1,32,8]{1,2,0:T(8,128)S(1)}, f32[1,32,8]{1,2,0:T(8,128)}, u32[]{:S(2)}) copy-start(f32[1,32,8]{1,2,0:T(8,128)} %param.8) | copy-start | bytes 3076
  6.0 33.8 %copy-start = (f32[1,128,768]{2,1,0:T(8,128)S(1)}, f32[1,128,768]{2,1,0:T(8,128)}, u32[]{:S(2)}) copy-start(f32[1,128,768]{2,1,0:T(8,128)} %param.11) | copy-start | bytes 1179652
  6.0 228.3 %all-to-all-start = ((bf16[64,8,2048]{2,1,0:T(8,128)(2,1)}), bf16[64,8,2048]{2,1,0:T(8,128)(2,1)S(1)}, u32[]{:S(2)}, u32[]{:S(2)}) async-start(bf16[64,8,2048]{2,1,0:T(8,128)(2,1)} %fusion.5), calls=%async_computation | async-start | bytes 4194304 | tf_op jit(solution)/shard_map/all_to_all | solution.py:68
  245.9 7.6 %copy-start.2 = (bf16[1,1,64,8,768]{4,3,2,1,0:T(8,128)(2,1)S(1)}, bf16[1,1,64,8,768]{4,3,2,1,0:T(8,128)(2,1)}, u32[]{:S(2)}) copy-start(bf16[1,1,64,8,768]{4,3,2,1,0:T(8,128)(2,1)} %param.6) | copy-start | bytes 2359300
  245.9 210.2 %all-to-all-start.1 = ((bf16[64,4,4224]{2,1,0:T(4,128)(2,1)}), bf16[64,4,4224]{2,1,0:T(4,128)(2,1)S(1)}, u32[]{:S(2)}, u32[]{:S(2)}) async-start(bf16[64,4,4224]{2,1,0:T(4,128)(2,1)} %pad_maximum_fusion.1), calls=%async_computation.1 | async-start | bytes 4325376 | tf_op jit(solution)/shard_map/all_to_all | solution.py:106
  458.6 5.1 copy-start.3
  511.3 2.5 copy-start.1
  511.3 2.5 copy-start.4

commit v11 on v8

--- a/solution.py
+++ b/solution.py
@@ -69,15 +69,18 @@
     selector = (
         position[:, None] == jnp.arange(experts * capacity, dtype=jnp.int32)[None, :]
     ).astype(jnp.bfloat16)
-    row_images = lax.dot_general(
-        selector,
-        returned.reshape(experts * capacity, model_width),
+    gate_rows = gate_weights.reshape(tok_rows, top_count)
+    gate_select = jnp.sum(
+        selector.astype(jnp.float32).reshape(tok_rows, top_count, experts * capacity)
+        * gate_rows[:, :, None],
+        axis=1,
+    )
+    tangent = lax.dot_general(
+        gate_select,
+        returned.reshape(experts * capacity, model_width).astype(jnp.float32),
         (((1,), (0,)), ((), ())),
+        precision=lax.Precision.HIGHEST,
         preferred_element_type=jnp.float32,
-    )
-    gate_rows = gate_weights.reshape(tok_rows, top_count)
-    tangent = jnp.sum(
-        gate_rows[:, :, None] * row_images.reshape(tok_rows, top_count, model_width), axis=1
     )
     weighted = (gate_rows[:, :, None] * tangent[:, None, :]).astype(jnp.bfloat16)
     outgoing = lax.dot_general(

time: 516 us -> 516 us (level)
  no operation moved by 1% of the time
where the time goes in v11:
time: 516 us; the launch traced here: 514 us
  blocking collectives  263 us (51%)
  waiting for transfers between devices  193 us (37%)
  starting transfers between devices  30.5 us (6%)
  matrix products  10.4 us (2%)
  other arithmetic  9.85 us (2%)
    all_to_all x1, blocking collectives, local(): lax.all_to_all(payload, EXPERT, split_axis=0, concat_axis=0, tiled=True)  217 us
    all_to_all x1, waiting for transfers between devices, local(): lax.all_to_all(images, EXPERT, split_axis=0, concat_axis=0, tiled=True)  193 us
    all_to_all x1, blocking collectives, local(): exchanged = lax.all_to_all(blocks, DP, 0, 0, tiled=True)  45.9 us
    all_to_all x1, starting transfers between devices, local(): lax.all_to_all(images, EXPERT, split_axis=0, concat_axis=0, tiled=True)  30.5 us
  transfers between devices with their start and end apart: 1, of which 1 were waited for; matrix products, arithmetic and copies ran while one was open for 1% of the time, Pallas kernels for 0%

profile of v11, /device:TPU:1, one launch (start us, length us, event | category | flops | bytes accessed | tf_op | source)
XLA Modules:
  0.0 514.4 jit_solution(6120374265751210735)
XLA Ops:
  0.6 0.0 copy-start
  0.6 1.1 copy-done
  1.8 5.1 fusion.6
  6.8 0.0 copy-start.5
  6.8 0.0 copy-start.4
  6.8 0.0 copy-start.2
  6.8 30.5 %all-to-all-start = ((bf16[64,8,2048]{2,1,0:T(8,128)(2,1)}), bf16[64,8,2048]{2,1,0:T(8,128)(2,1)S(1)}, u32[]{:S(2)}, u32[]{:S(2)}) async-start(bf16[64,8,2048]{2,1,0:T(8,128)(2,1)} %fusion.6), calls=%async_computation | async-start | bytes 4194304 | tf_op jit(solution)/shard_map/all_to_all | solution.py:68
  37.4 0.0 copy-done.5
  37.4 0.1 copy.32
  37.5 0.1 reshape.99
  37.6 0.1 eq.46
  37.7 0.0 copy-done.4
  37.7 0.1 copy.35
  37.7 0.1 copy.37
  37.8 0.1 mul.102
  37.9 0.6 reduce-window.6
  38.5 0.2 slice_reduce_fusion
  38.8 0.1 fusion.25
  38.9 0.1 reduce_sum.75
  39.0 1.7 fusion.18
  40.6 0.9 multiply_reduce_fusion
  41.5 0.0 copy-done.2
  41.5 0.7 multiply_reduce_fusion.1
  42.2 192.9 %all-to-all-done = bf16[64,8,2048]{2,1,0:T(8,128)(2,1)S(1)} async-done(((bf16[64,8,2048]{2,1,0:T(8,128)(2,1)}), bf16[64,8,2048]{2,1,0:T(8,128)(2,1)S(1)}, u32[]{:S(2)}, u32[]{:S(2)}) %all-to-all-start) | async-done | bytes 2097184 | tf_op jit(solution)/shard_map/all_to_all | solution.py:68
  235.1 2.6 multiply_reduce_fusion.2
  239.1 0.7 reduce-precision_convert_fusion.1
  239.8 0.1 maximum_bitcast_fusion
  239.9 0.8 fusion.5
  240.8 0.2 pad_maximum_fusion.1
  240.9 217.1 %all_to_all.15 = bf16[64,8,2176]{2,1,0:T(8,128)(2,1)S(1)} all-to-all(bf16[64,8,2176]{2,1,0:T(8,128)(2,1)S(1)} %pad_maximum_fusion.1), channel_id=1, replica_groups=mesh['expert_0'=32,'expert_1'=2,'dp_0'=4,'dp_1'=4] {'expert_0','expert_1'}, dimensions={0} | all-to-all | bytes 4456448 | tf_op jit(solution)/shard_map/all_to_all | solution.py:100
  458.0 0.1 fusion.27
  458.1 0.1 maximum_bitcast_fusion.1
  458.2 1.9 convolution_convert_fusion
  460.1 0.2 pad_maximum_fusion
  460.3 45.9 %all_to_all.16 = bf16[16,136,768]{2,1,0:T(8,128)(2,1)S(1)} all-to-all(bf16[16,136,768]{2,1,0:T(8,128)(2,1)S(1)} %pad_maximum_fusion), channel_id=1, replica_groups=mesh['expert_0'=32,'expert_1'=2,'dp_0'=4,'dp_1'=4] {'dp_0','dp_1'}, dimensions={0} | all-to-all | bytes 6684672 | tf_op jit(solution)/shard_map/all_to_all | solution.py:112
  506.3 0.0 copy-start.1
  506.3 1.7 copy-done.1
  508.0 0.0 copy-start.3
  508.0 0.1 copy.39
  508.1 0.1 add_reduce_fusion
  508.2 0.6 fusion.30
  510.1 2.4 convert_reduce_fusion
  512.5 0.0 copy-done.3
  512.5 1.9 fusion.21
  (13 shorter events, 0.2 us)
Async XLA Ops:
  0.6 1.1 copy-start
  6.8 30.6 %copy-start.5 = (s32[1,32,8]{1,2,0:T(8,128)S(1)}, s32[1,32,8]{1,2,0:T(8,128)}, u32[]{:S(2)}) copy-start(s32[1,32,8]{1,2,0:T(8,128)} %param.7) | copy-start | bytes 3076
  6.8 30.8 %copy-start.4 = (f32[1,32,8]{1,2,0:T(8,128)S(1)}, f32[1,32,8]{1,2,0:T(8,128)}, u32[]{:S(2)}) copy-start(f32[1,32,8]{1,2,0:T(8,128)} %param.8) | copy-start | bytes 3076
  6.8 34.7 %copy-start.2 = (f32[1,128,768]{2,1,0:T(8,128)S(1)}, f32[1,128,768]{2,1,0:T(8,128)}, u32[]{:S(2)}) copy-start(f32[1,128,768]{2,1,0:T(8,128)} %param.11) | copy-start | bytes 1179652
  6.8 228.3 %all-to-all-start = ((bf16[64,8,2048]{2,1,0:T(8,128)(2,1)}), bf16[64,8,2048]{2,1,0:T(8,128)(2,1)S(1)}, u32[]{:S(2)}, u32[]{:S(2)}) async-start(bf16[64,8,2048]{2,1,0:T(8,128)(2,1)} %fusion.6), calls=%async_computation | async-start | bytes 4194304 | tf_op jit(solution)/shard_map/all_to_all | solution.py:68
  506.3 1.7 copy-start.1
  508.0 4.5 copy-start.3
